TPU v7x, 768 devices: a whole 4x8x12 slice. The times are simulated.
768 devices in a mesh: wave: 48 (over x, z), lev: 16 (over y, core).
Axes of the slice: x: 4, y: 8, z: 12, core: 2. Of those that a mesh axis runs over, the one named last changes fastest.
Arguments:
- spectral: bfloat16 [96, 768, 1280], P('lev', 'wave'), may hold values from -0.19921875 to 0.19921875
- legendre: bfloat16 [768, 768, 1280], P('wave', 'lev'), may hold values from -0.15625 to 0.15625
- weights: float32 [768], replicated, may hold values from 4 to 40
- nlon: int32 [768], replicated, may hold values from 20 to 5136, as said below
- assignment: int32 [768], replicated, may hold values from 1 to 1279, as said below
Outputs:
- tendencies: float32 [96, 768, 1280], P('lev', 'wave')
Inputs may be any that keep to these rules, and one draw needn't show every extreme that they name: `assignment`: slots 2 i and 2 i + 1 hold m and 1280 - m for some m with 1 <= m < 640; all values are distinct, and m = 1 is always among them. `nlon`: each count is 20 plus four times a whole number; both ends of the range occur in every draw.
All inputs are finite; a program needn't handle non-finite values.
Results may differ from a plain program's by a relative error of at most 0.018.
Values may be sent and summed in bfloat16 or wider, within the bound.
No kernel may reach another device: no remote copies, remote signals or barrier semaphores. Data moves between devices by JAX's collectives and lax.ppermute only.
A program may use at most 32 MiB of HBM per device.

v0:
```python
import math

import jax
import jax.numpy as jnp
from jax import lax
from jax.sharding import PartitionSpec as P

TRUNC = 1279
LON_BLOCK = 768
NLONPAD = 5376


def angle_parts(count, waves, starts):
    phase = starts[:, None] % count * waves[None, :] % count
    angle = 2.0 * math.pi * phase.astype(jnp.float32) / count.astype(jnp.float32)
    return (jnp.cos(angle), jnp.sin(angle))


def compose_table(count, waves, coarse_cos, coarse_sin, fine_cos, fine_sin, lon_rows):
    cosine = (
        coarse_cos[:, None, :] * fine_cos[None, :, :]
        - coarse_sin[:, None, :] * fine_sin[None, :, :]
    )
    sine = (
        coarse_sin[:, None, :] * fine_cos[None, :, :]
        + coarse_cos[:, None, :] * fine_sin[None, :, :]
    )
    rows_total = lon_rows.shape[0]
    cosine = cosine.reshape(rows_total, waves.shape[0])
    sine = sine.reshape(rows_total, waves.shape[0])
    usable = (lon_rows[:, None] < count) & (2 * waves[None, :] < count)
    cosine = jnp.where(usable, cosine, jnp.zeros((), jnp.float32))
    sine = jnp.where(usable, -sine, jnp.zeros((), jnp.float32))
    return jnp.concatenate([cosine, sine], axis=1).astype(jnp.bfloat16)


def quadratic(grid):
    fields = grid.reshape(grid.shape[0], grid.shape[1] // 3, 3)
    vort = fields[:, :, 0]
    diverg = fields[:, :, 1]
    temper = fields[:, :, 2]
    stacked = jnp.stack([vort * temper, diverg * temper, vort * diverg], axis=-1)
    return stacked.reshape(grid.shape[0], grid.shape[1]).astype(jnp.bfloat16)


def per_device(spectral, legendre, weights, nlon, assignment):
    wave_index = lax.axis_index("wave")
    lev_index = lax.axis_index("lev")
    slots = legendre.shape[0]
    lat_band = legendre.shape[1]
    kmax_width = legendre.shape[2]
    all_slots = assignment.shape[0]
    own_waves = lax.dynamic_slice_in_dim(assignment, wave_index * slots, slots)
    krange = lax.iota(jnp.int32, kmax_width)
    live_rows = krange[None, :] <= (TRUNC - own_waves)[:, None]
    local = jnp.where(live_rows[None], spectral, jnp.zeros((), jnp.bfloat16))
    spec_all = lax.all_gather(local, "lev", axis=0, tiled=True)
    columns = spec_all.shape[0]
    four_local = jnp.einsum(
        "mlk,cmk->mlc", legendre, spec_all, preferred_element_type=jnp.float32
    ).astype(jnp.bfloat16)
    fourier = lax.all_to_all(four_local, "wave", split_axis=1, concat_axis=0, tiled=True)
    mine = fourier.shape[1]
    half_cols = columns // 2
    fine_rows = lax.iota(jnp.int32, 128)
    coarse_rows = lax.iota(jnp.int32, NLONPAD // 128) * 128
    coarse_step = LON_BLOCK // 128
    lat_index = lev_index * lat_band + wave_index * mine + 0
    count = lax.dynamic_slice_in_dim(nlon, lat_index, 1)[0]
    weight = lax.dynamic_slice_in_dim(weights, lat_index, 1)[0]
    pairs = fourier[:, 0, :].reshape(all_slots, half_cols, 2)
    stacked = jnp.concatenate([pairs[:, :, 0], pairs[:, :, 1]], axis=0)
    fine_cos, fine_sin = angle_parts(count, assignment, fine_rows)
    coarse_cos_all, coarse_sin_all = angle_parts(count, assignment, coarse_rows)

    def lon_block(block_step, total):
        lon_rows = block_step * LON_BLOCK + lax.iota(jnp.int32, LON_BLOCK)
        coarse_cos = lax.dynamic_slice_in_dim(coarse_cos_all, block_step * coarse_step, coarse_step)
        coarse_sin = lax.dynamic_slice_in_dim(coarse_sin_all, block_step * coarse_step, coarse_step)
        table = compose_table(
            count, assignment, coarse_cos, coarse_sin, fine_cos, fine_sin, lon_rows
        )
        grid = 2.0 * jnp.dot(table, stacked, preferred_element_type=jnp.float32)
        products = quadratic(grid)
        return total + lax.dot_general(
            table, products, (((0,), (0,)), ((), ())), preferred_element_type=jnp.float32
        )

    start_total = jnp.zeros((2 * all_slots, half_cols), jnp.float32)
    total = lax.fori_loop(0, NLONPAD // LON_BLOCK, lon_block, start_total)
    back = total * (weight / count.astype(jnp.float32))
    joined = jnp.stack([back[:all_slots], back[all_slots:]], axis=-1).reshape(all_slots, columns)
    analysed_rows = [joined.astype(jnp.bfloat16)]
    analysed = jnp.stack(analysed_rows, axis=1)
    returned = lax.all_to_all(analysed, "wave", split_axis=0, concat_axis=1, tiled=True)
    band_term = jnp.einsum("mlc,mlk->cmk", returned, legendre, preferred_element_type=jnp.float32)
    band_term = jnp.where(live_rows[None], band_term, jnp.zeros((), jnp.float32))
    return lax.psum_scatter(
        band_term.astype(jnp.bfloat16), "lev", scatter_dimension=0, tiled=True
    ).astype(jnp.float32)


def solution(mesh):
    return jax.shard_map(
        per_device,
        mesh=mesh,
        in_specs=(P("lev", "wave", None), P("wave", "lev", None), P(), P(), P()),
        out_specs=P("lev", "wave", None),
        check_vma=False,
    )
```

profile of v0, /device:TPU:1, one launch (start us, length us, event | category | flops | bytes accessed | tf_op | source)
XLA Modules:
  0.0 284.8 jit_solution(14471927226797883278)
XLA Ops:
  7.5 1.7 broadcast_select_fusion
  9.2 1.3 dynamic_slice.24
  12.6 1.3 dynamic_slice.25
  14.6 50.1 %all-gather.2.cloned.1.call-done = bf16[96,16,1280]{2,1,0:T(8,128)(2,1)} async-done(((bf16[6,16,1280]{2,1,0:T(8,128)(2,1)}), bf16[96,16,1280]{2,1,0:T(8,128)(2,1)}) %all-gather.2.cloned.1.call-update) | async-done | bytes 3932176 | tf_op jit(solution)/shard_map/all_gather | solution.py:57
  64.7 3.4 %fusion.25 = bf16[16,48,96]{2,1,0:T(8,128)(2,1)S(1)} fusion(bf16[16,48,1280]{2,1,0:T(8,128)(2,1)S(1)} %copy-done, bf16[96,16,1280]{2,1,0:T(8,128)(2,1)} %all-gather.2.cloned.1.call-done), kind=kOutput, calls=%fused_computation.38 | convolution fusion | flops 188817408 | bytes 6045696 | tf_op jit(solution)/shard_map/mlk,cmk->mlc/dot_general | solution.py:59
  68.8 13.0 %all-to-all-start = ((bf16[16,48,96]{2,0,1:T(8,128)(2,1)}), bf16[16,48,96]{2,0,1:T(8,128)(2,1)S(1)}, u32[]{:S(2)}, u32[]{:S(2)}) async-start(bf16[16,48,96]{2,0,1:T(8,128)(2,1)} %copy.31), calls=%async_computation | async-start | bytes 393216 | tf_op jit(solution)/shard_map/all_to_all | solution.py:62
  82.2 2.7 fusion.37
  84.9 11.4 %all-to-all-done = bf16[16,48,96]{2,0,1:T(8,128)(2,1)S(1)} async-done(((bf16[16,48,96]{2,0,1:T(8,128)(2,1)}), bf16[16,48,96]{2,0,1:T(8,128)(2,1)S(1)}, u32[]{:S(2)}, u32[]{:S(2)}) %all-to-all-start) | async-done | bytes 147488 | tf_op jit(solution)/shard_map/all_to_all | solution.py:62
  99.2 91.2 %while.16 = (s32[]{:T(128)}, f32[1536,48]{0,1:T(8,128)}, s32[]{:T(128)}, s32[768]{0:T(1024)S(1)}, f32[42,768]{1,0:T(8,128)}, /*index=5*/f32[42,768]{1,0:T(8,128)...) while((s32[]{:T(128)}, f32[1536,48]{0,1:T(8,128)}, ...), condition=%wide.region_1.2_spmd.clone.clone.clone, body=%wide.region_0.1_spmd.clone.clone.clone.sunk | while | flops 244571136 | bytes 21600100 | solution.py:90
  100.8 5.3 %fusion.51 = (f32[128,768]{1,0:T(8,128)S(1)}, f32[128,768]{1,0:T(8,128)S(1)}) fusion(f32[]{:T(128)} %get-tuple-element.516, pred[]{:T(512)} %get-tuple-element.513, s32[]{:T(128)} %get-tuple-element.515, s32[768]{0:T(1024)S(1)} %get-tuple-element.509, s32[128]{0:T(128)S(1)} %get-tuple-element.514), kind=kLoop, calls=%fused_computation.22.clone.1 | loop fusion | flops 1081344 | bytes 790025 | tf_op jit(solution)/shard_map/cos | solution.py:16
  107.4 1.0 copy-done.1
  109.7 2.5 convolution_add_fusion.2
  113.8 5.3 %fusion.51 = (f32[128,768]{1,0:T(8,128)S(1)}, f32[128,768]{1,0:T(8,128)S(1)}) fusion(f32[]{:T(128)} %get-tuple-element.516, pred[]{:T(512)} %get-tuple-element.513, s32[]{:T(128)} %get-tuple-element.515, s32[768]{0:T(1024)S(1)} %get-tuple-element.509, s32[128]{0:T(128)S(1)} %get-tuple-element.514), kind=kLoop, calls=%fused_computation.22.clone.1 | loop fusion | flops 1081344 | bytes 790025 | tf_op jit(solution)/shard_map/cos | solution.py:16
  120.4 1.0 copy-done.1
  122.7 2.5 convolution_add_fusion.2
  126.8 5.3 %fusion.51 = (f32[128,768]{1,0:T(8,128)S(1)}, f32[128,768]{1,0:T(8,128)S(1)}) fusion(f32[]{:T(128)} %get-tuple-element.516, pred[]{:T(512)} %get-tuple-element.513, s32[]{:T(128)} %get-tuple-element.515, s32[768]{0:T(1024)S(1)} %get-tuple-element.509, s32[128]{0:T(128)S(1)} %get-tuple-element.514), kind=kLoop, calls=%fused_computation.22.clone.1 | loop fusion | flops 1081344 | bytes 790025 | tf_op jit(solution)/shard_map/cos | solution.py:16
  133.4 1.0 copy-done.1
  135.8 2.5 convolution_add_fusion.2
  139.8 5.3 %fusion.51 = (f32[128,768]{1,0:T(8,128)S(1)}, f32[128,768]{1,0:T(8,128)S(1)}) fusion(f32[]{:T(128)} %get-tuple-element.516, pred[]{:T(512)} %get-tuple-element.513, s32[]{:T(128)} %get-tuple-element.515, s32[768]{0:T(1024)S(1)} %get-tuple-element.509, s32[128]{0:T(128)S(1)} %get-tuple-element.514), kind=kLoop, calls=%fused_computation.22.clone.1 | loop fusion | flops 1081344 | bytes 790025 | tf_op jit(solution)/shard_map/cos | solution.py:16
  146.5 1.0 copy-done.1
  148.8 2.5 convolution_add_fusion.2
  152.9 5.3 %fusion.51 = (f32[128,768]{1,0:T(8,128)S(1)}, f32[128,768]{1,0:T(8,128)S(1)}) fusion(f32[]{:T(128)} %get-tuple-element.516, pred[]{:T(512)} %get-tuple-element.513, s32[]{:T(128)} %get-tuple-element.515, s32[768]{0:T(1024)S(1)} %get-tuple-element.509, s32[128]{0:T(128)S(1)} %get-tuple-element.514), kind=kLoop, calls=%fused_computation.22.clone.1 | loop fusion | flops 1081344 | bytes 790025 | tf_op jit(solution)/shard_map/cos | solution.py:16
  161.9 2.5 convolution_add_fusion.2
  165.9 5.3 %fusion.51 = (f32[128,768]{1,0:T(8,128)S(1)}, f32[128,768]{1,0:T(8,128)S(1)}) fusion(f32[]{:T(128)} %get-tuple-element.516, pred[]{:T(512)} %get-tuple-element.513, s32[]{:T(128)} %get-tuple-element.515, s32[768]{0:T(1024)S(1)} %get-tuple-element.509, s32[128]{0:T(128)S(1)} %get-tuple-element.514), kind=kLoop, calls=%fused_computation.22.clone.1 | loop fusion | flops 1081344 | bytes 790025 | tf_op jit(solution)/shard_map/cos | solution.py:16
  174.9 2.5 convolution_add_fusion.2
  179.0 5.3 %fusion.51 = (f32[128,768]{1,0:T(8,128)S(1)}, f32[128,768]{1,0:T(8,128)S(1)}) fusion(f32[]{:T(128)} %get-tuple-element.516, pred[]{:T(512)} %get-tuple-element.513, s32[]{:T(128)} %get-tuple-element.515, s32[768]{0:T(1024)S(1)} %get-tuple-element.509, s32[128]{0:T(128)S(1)} %get-tuple-element.514), kind=kLoop, calls=%fused_computation.22.clone.1 | loop fusion | flops 1081344 | bytes 790025 | tf_op jit(solution)/shard_map/cos | solution.py:16
  187.9 2.5 convolution_add_fusion.2
  193.4 17.8 %all_to_all.33 = bf16[48,2,768]{2,1,0:T(2,128)(2,1)S(1)} all-to-all(bf16[48,2,768]{2,1,0:T(2,128)(2,1)S(1)} %reshape.138), channel_id=1, replica_groups=mesh['wave'=48,'lev'=16] {'wave'}, dimensions={0} | all-to-all | bytes 294912 | tf_op jit(solution)/shard_map/all_to_all | solution.py:95
  211.5 1.2 fusion.21
  212.8 4.0 %copy.37 = bf16[96,16,1280]{2,1,0:T(8,128)(2,1)} copy(bf16[96,16,1280]{2,0,1:T(8,128)(2,1)S(1)} %fusion.21) | data formatting | bytes 7864320 | tf_op jit(solution)/shard_map/convert_element_type | solution.py:99
  216.8 59.4 %reduce-scatter.2.cloned.1.call-done = bf16[6,16,1280]{2,1,0:T(8,128)(2,1)} async-done(((bf16[96,16,1280]{2,1,0:T(8,128)(2,1)}), bf16[6,16,1280]{2,1,0:T(8,128)(2,1)}) %reduce-scatter.2.cloned.1.call-update) | async-done | bytes 245776 | tf_op jit(solution)/shard_map/reduce_scatter | solution.py:98
  276.2 1.8 convert_element_type.58
  (146 shorter events, 40.0 us)
Async XLA Ops:
  6.5 58.2 %copy-start = (bf16[16,48,1280]{2,1,0:T(8,128)(2,1)S(1)}, bf16[16,48,1280]{2,1,0:T(8,128)(2,1)}, u32[]{:S(2)}) copy-start(bf16[16,48,1280]{2,1,0:T(8,128)(2,1)} %param.8) | copy-start | bytes 5898244
  6.5 58.2 %all-gather.2.cloned.1.call-start = ((), (), s32[]{:S(2)}) async-start(), calls=%async_computation.3 | async-start | bytes 4177920 | tf_op jit(solution)/shard_map/all_gather | solution.py:57
  14.6 67.6 %copy-start.2 = (s32[768]{0:T(1024)S(1)}, s32[768]{0:T(1024)}, u32[]{:S(2)}) copy-start(s32[768]{0:T(1024)} %param.11) | copy-start | bytes 9220
  68.8 27.4 %all-to-all-start = ((bf16[16,48,96]{2,0,1:T(8,128)(2,1)}), bf16[16,48,96]{2,0,1:T(8,128)(2,1)S(1)}, u32[]{:S(2)}, u32[]{:S(2)}) async-start(bf16[16,48,96]{2,0,1:T(8,128)(2,1)} %copy.31), calls=%async_computation | async-start | bytes 393216 | tf_op jit(solution)/shard_map/all_to_all | solution.py:62
  81.8 194.4 %reduce-scatter.2.cloned.1.call-start = ((), (), s32[]{:S(2)}) async-start(), calls=%async_computation.4 | async-start | bytes 4177920 | tf_op jit(solution)/shard_map/reduce_scatter | solution.py:98
  99.2 8.1 %copy-start.3 = (f32[42,768]{1,0:T(8,128)}, f32[42,768]{1,0:T(8,128)S(1)}, u32[]{:S(2)}) copy-start(f32[42,768]{1,0:T(8,128)S(1)} %get-tuple-element.511) | copy-start | bytes 387076 | tf_op jit(solution)/shard_map/while
  106.7 1.7 copy-start.5
  107.4 1.1 copy-start.1
  109.3 2.9 %copy-start.4 = (f32[42,768]{1,0:T(8,128)S(1)}, f32[42,768]{1,0:T(8,128)}, u32[]{:S(2)}) copy-start(f32[42,768]{1,0:T(8,128)} %copy-done.3) | copy-start | bytes 387076 | tf_op jit(solution)/shard_map/while
  112.2 8.1 %copy-start.3 = (f32[42,768]{1,0:T(8,128)}, f32[42,768]{1,0:T(8,128)S(1)}, u32[]{:S(2)}) copy-start(f32[42,768]{1,0:T(8,128)S(1)} %get-tuple-element.511) | copy-start | bytes 387076 | tf_op jit(solution)/shard_map/while
  119.7 1.7 copy-start.5
  120.4 1.1 copy-start.1
  122.3 3.0 %copy-start.4 = (f32[42,768]{1,0:T(8,128)S(1)}, f32[42,768]{1,0:T(8,128)}, u32[]{:S(2)}) copy-start(f32[42,768]{1,0:T(8,128)} %copy-done.3) | copy-start | bytes 387076 | tf_op jit(solution)/shard_map/while
  125.3 8.1 %copy-start.3 = (f32[42,768]{1,0:T(8,128)}, f32[42,768]{1,0:T(8,128)S(1)}, u32[]{:S(2)}) copy-start(f32[42,768]{1,0:T(8,128)S(1)} %get-tuple-element.511) | copy-start | bytes 387076 | tf_op jit(solution)/shard_map/while
  132.8 1.7 copy-start.5
  133.4 1.1 copy-start.1
  135.4 3.0 %copy-start.4 = (f32[42,768]{1,0:T(8,128)S(1)}, f32[42,768]{1,0:T(8,128)}, u32[]{:S(2)}) copy-start(f32[42,768]{1,0:T(8,128)} %copy-done.3) | copy-start | bytes 387076 | tf_op jit(solution)/shard_map/while
  138.3 8.1 %copy-start.3 = (f32[42,768]{1,0:T(8,128)}, f32[42,768]{1,0:T(8,128)S(1)}, u32[]{:S(2)}) copy-start(f32[42,768]{1,0:T(8,128)S(1)} %get-tuple-element.511) | copy-start | bytes 387076 | tf_op jit(solution)/shard_map/while
  145.8 1.7 copy-start.5
  146.5 1.1 copy-start.1
  148.4 3.0 %copy-start.4 = (f32[42,768]{1,0:T(8,128)S(1)}, f32[42,768]{1,0:T(8,128)}, u32[]{:S(2)}) copy-start(f32[42,768]{1,0:T(8,128)} %copy-done.3) | copy-start | bytes 387076 | tf_op jit(solution)/shard_map/while
  151.4 8.1 %copy-start.3 = (f32[42,768]{1,0:T(8,128)}, f32[42,768]{1,0:T(8,128)S(1)}, u32[]{:S(2)}) copy-start(f32[42,768]{1,0:T(8,128)S(1)} %get-tuple-element.511) | copy-start | bytes 387076 | tf_op jit(solution)/shard_map/while
  158.8 1.7 copy-start.5
  159.5 1.1 copy-start.1
  161.4 3.0 %copy-start.4 = (f32[42,768]{1,0:T(8,128)S(1)}, f32[42,768]{1,0:T(8,128)}, u32[]{:S(2)}) copy-start(f32[42,768]{1,0:T(8,128)} %copy-done.3) | copy-start | bytes 387076 | tf_op jit(solution)/shard_map/while
  164.4 8.1 %copy-start.3 = (f32[42,768]{1,0:T(8,128)}, f32[42,768]{1,0:T(8,128)S(1)}, u32[]{:S(2)}) copy-start(f32[42,768]{1,0:T(8,128)S(1)} %get-tuple-element.511) | copy-start | bytes 387076 | tf_op jit(solution)/shard_map/while
  171.9 1.7 copy-start.5
  172.5 1.1 copy-start.1
  174.5 3.0 %copy-start.4 = (f32[42,768]{1,0:T(8,128)S(1)}, f32[42,768]{1,0:T(8,128)}, u32[]{:S(2)}) copy-start(f32[42,768]{1,0:T(8,128)} %copy-done.3) | copy-start | bytes 387076 | tf_op jit(solution)/shard_map/while
  177.4 8.1 %copy-start.3 = (f32[42,768]{1,0:T(8,128)}, f32[42,768]{1,0:T(8,128)S(1)}, u32[]{:S(2)}) copy-start(f32[42,768]{1,0:T(8,128)S(1)} %get-tuple-element.511) | copy-start | bytes 387076 | tf_op jit(solution)/shard_map/while
  184.9 1.7 copy-start.5
  187.5 3.0 %copy-start.4 = (f32[42,768]{1,0:T(8,128)S(1)}, f32[42,768]{1,0:T(8,128)}, u32[]{:S(2)}) copy-start(f32[42,768]{1,0:T(8,128)} %copy-done.3) | copy-start | bytes 387076 | tf_op jit(solution)/shard_map/while
  (1 other events, 1.1 us)
Sparse Core Ops, SparseCore 0:
  9.7 54.9 all-gather.1
  216.9 59.2 reduce-scatter.1
where the time goes:
time: 286 us; the launch traced here: 285 us
  waiting for transfers between devices  121 us (42%)
  other arithmetic  62.1 us (22%)
  matrix products  28.1 us (10%)
  local copies, waits for them, and re-layouts  25.9 us (9%)
  blocking collectives  17.8 us (6%)
  between operations  16.2 us (6%)
  starting transfers between devices  13 us (5%)
    reduce_scatter x1, waiting for transfers between devices, per_device(): lax.psum_scatter(band_term.astype(jnp.bfloat16), 'lev', scatter_dimension...  59.4 us
    all_gather x1, waiting for transfers between devices, per_device(): spec_all = lax.all_gather(local, 'lev', axis=0, tiled=True)  50.1 us
    cos x7, other arithmetic, angle_parts(): return (jnp.cos(angle), jnp.sin(angle))  36.8 us
    all_to_all x1, blocking collectives, per_device(): lax.all_to_all(analysed, 'wave', split_axis=0, concat_axis=1, tiled=True)  17.8 us
    dot_general x7, matrix products, lon_block(): lax.dot_general(table, products, (((0,), (0,)), ((), ())), preferred_elem...  17.8 us
    all_to_all x1, starting transfers between devices, per_device(): lax.all_to_all(four_local, 'wave', split_axis=1, concat_axis=0, tiled=True)  13 us
    all_to_all x1, waiting for transfers between devices, per_device(): lax.all_to_all(four_local, 'wave', split_axis=1, concat_axis=0, tiled=True)  11.4 us
    while x56, local copies, waits for them, and re-layouts  7.41 us
  transfers between devices with their start and end apart: 3, of which 3 were waited for; matrix products, arithmetic and copies ran while one was open for 2% of the time, Pallas kernels for 0%

commit v1 on v0

--- a/solution.py
+++ b/solution.py
@@ -50,15 +50,22 @@
     lat_band = legendre.shape[1]
     kmax_width = legendre.shape[2]
     all_slots = assignment.shape[0]
+    pairs_n = slots // 2
     own_waves = lax.dynamic_slice_in_dim(assignment, wave_index * slots, slots)
     krange = lax.iota(jnp.int32, kmax_width)
-    live_rows = krange[None, :] <= (TRUNC - own_waves)[:, None]
-    local = jnp.where(live_rows[None], spectral, jnp.zeros((), jnp.bfloat16))
-    spec_all = lax.all_gather(local, "lev", axis=0, tiled=True)
+    front = krange[None, :] < (kmax_width - own_waves.reshape(pairs_n, 2)[:, 0])[:, None]
+    leg_pairs = legendre.reshape(pairs_n, 2, lat_band, kmax_width)
+    zero_bf = jnp.zeros((), jnp.bfloat16)
+    leg_a = jnp.where(front[:, None, :], leg_pairs[:, 0], zero_bf)
+    leg_b = jnp.where(front[:, None, :], zero_bf, leg_pairs[:, 1, :, ::-1])
+    packed_leg = jnp.stack([leg_a, leg_b], axis=1)
+    spec_pairs = spectral.reshape(spectral.shape[0], pairs_n, 2, kmax_width)
+    packed_spec = jnp.where(front[None], spec_pairs[:, :, 0], spec_pairs[:, :, 1, ::-1])
+    spec_all = lax.all_gather(packed_spec, "lev", axis=0, tiled=True)
     columns = spec_all.shape[0]
     four_local = jnp.einsum(
-        "mlk,cmk->mlc", legendre, spec_all, preferred_element_type=jnp.float32
-    ).astype(jnp.bfloat16)
+        "pxlk,cpk->pxlc", packed_leg, spec_all, preferred_element_type=jnp.float32
+    ).astype(jnp.bfloat16).reshape(slots, lat_band, columns)
     fourier = lax.all_to_all(four_local, "wave", split_axis=1, concat_axis=0, tiled=True)
     mine = fourier.shape[1]
     half_cols = columns // 2
@@ -93,11 +100,19 @@
     analysed_rows = [joined.astype(jnp.bfloat16)]
     analysed = jnp.stack(analysed_rows, axis=1)
     returned = lax.all_to_all(analysed, "wave", split_axis=0, concat_axis=1, tiled=True)
-    band_term = jnp.einsum("mlc,mlk->cmk", returned, legendre, preferred_element_type=jnp.float32)
-    band_term = jnp.where(live_rows[None], band_term, jnp.zeros((), jnp.float32))
-    return lax.psum_scatter(
+    returned = returned.reshape(pairs_n, 2, lat_band, columns)
+    band_term = jnp.einsum(
+        "pxlc,pxlk->cpk", returned, packed_leg, preferred_element_type=jnp.float32
+    )
+    summed = lax.psum_scatter(
         band_term.astype(jnp.bfloat16), "lev", scatter_dimension=0, tiled=True
-    ).astype(jnp.float32)
+    )
+    zero_f = jnp.zeros((), jnp.float32)
+    summed = summed.astype(jnp.float32)
+    out_a = jnp.where(front[None], summed, zero_f)
+    out_b = jnp.where(front[None], zero_f, summed)[:, :, ::-1]
+    out = jnp.stack([out_a, out_b], axis=2)
+    return out.reshape(summed.shape[0], slots, kmax_width)
 
 
 def solution(mesh):

time: 286 us -> 276 us (0.965)
  waiting for transfers between devices: 121 us -> 113 us
    all_gather x1, waiting for transfers between devices: 50.1 us -> 44.2 us  [per_device(): spec_all = lax.all_gather(packed_spec, 'lev', axis=0, tiled=True)]
    dynamic_slice x7, local copies, waits for them, and re-layouts: 5.73 us -> 0.11 us  [lon_block(): lax.dynamic_slice_in_dim(coarse_sin_all, block_step * coarse_step, coarse...]
    rev x0 -> x3, local copies, waits for them, and re-layouts: none -> 3.97 us  [the longest x1 1.83 us: per_device(): spec_pairs[:, :, 1, ::-1]]
    reshape x0 -> x4, local copies, waits for them, and re-layouts: none -> 2.97 us  [the longest x1 1.12 us: per_device(): return out.reshape(summed.shape[0], slots, kmax_width)]
    reduce_scatter x1, waiting for transfers between devices: 59.4 us -> 56.5 us  [per_device(): lax.psum_scatter(band_term.astype(jnp.bfloat16), 'lev', scatter_dimension...]
    another operation x15 -> x17, other arithmetic: 6.35 us -> 7.19 us
    while x56 -> x112, local copies, waits for them, and re-layouts: 7.41 us -> 7.54 us
  transfers between devices with their start and end apart: 3 -> 3, of which waited for: 3 -> 3; matrix products, arithmetic and copies ran while one was open for 2% -> 3% of each run, Pallas kernels for 0% -> 0%
where the time goes in v1:
time: 276 us; the launch traced here: 275 us
  waiting for transfers between devices  113 us (41%)
  other arithmetic  60.3 us (22%)
  matrix products  26.9 us (10%)
  local copies, waits for them, and re-layouts  26.4 us (10%)
  blocking collectives  17.8 us (6%)
  between operations  16.2 us (6%)
  starting transfers between devices  13 us (5%)
    reduce_scatter x1, waiting for transfers between devices, per_device(): lax.psum_scatter(band_term.astype(jnp.bfloat16), 'lev', scatter_dimension...  56.5 us
    all_gather x1, waiting for transfers between devices, per_device(): spec_all = lax.all_gather(packed_spec, 'lev', axis=0, tiled=True)  44.2 us
    cos x7, other arithmetic, angle_parts(): return (jnp.cos(angle), jnp.sin(angle))  36.9 us
    dot_general x7, matrix products, lon_block(): lax.dot_general(table, products, (((0,), (0,)), ((), ())), preferred_elem...  18.2 us
    all_to_all x1, blocking collectives, per_device(): lax.all_to_all(analysed, 'wave', split_axis=0, concat_axis=1, tiled=True)  17.8 us
    all_to_all x1, starting transfers between devices, per_device(): lax.all_to_all(four_local, 'wave', split_axis=1, concat_axis=0, tiled=True)  13 us
    all_to_all x1, waiting for transfers between devices, per_device(): lax.all_to_all(four_local, 'wave', split_axis=1, concat_axis=0, tiled=True)  12 us
    while x112, local copies, waits for them, and re-layouts  7.54 us
  transfers between devices with their start and end apart: 3, of which 3 were waited for; matrix products, arithmetic and copies ran while one was open for 3% of the time, Pallas kernels for 0%

profile of v1, /device:TPU:1, one launch (start us, length us, event | category | flops | bytes accessed | tf_op | source)
XLA Modules:
  0.0 274.6 jit_solution(6698892133874070901)
XLA Ops:
  9.0 1.8 rev.10
  11.5 1.3 dynamic_slice.24
  14.1 1.6 slice_select_fusion
  15.8 1.4 rev.9
  17.8 1.3 dynamic_slice.25
  19.9 44.2 %all-gather.2.cloned.1.call-done = bf16[96,8,1280]{2,1,0:T(8,128)(2,1)} async-done(((bf16[6,8,1280]{2,1,0:T(8,128)(2,1)}), bf16[96,8,1280]{2,1,0:T(8,128)(2,1)}) %all-gather.2.cloned.1.call-update) | async-done | bytes 1966096 | tf_op jit(solution)/shard_map/all_gather | solution.py:64
  64.0 2.3 fusion.22
  67.0 13.0 %all-to-all-start = ((bf16[16,48,96]{2,0,1:T(8,128)(2,1)}), bf16[16,48,96]{2,0,1:T(8,128)(2,1)S(1)}, u32[]{:S(2)}, u32[]{:S(2)}) async-start(bf16[16,48,96]{2,0,1:T(8,128)(2,1)} %copy.51), calls=%async_computation | async-start | bytes 393216 | tf_op jit(solution)/shard_map/all_to_all | solution.py:69
  80.3 2.1 fusion.33
  82.4 12.0 %all-to-all-done = bf16[16,48,96]{2,0,1:T(8,128)(2,1)S(1)} async-done(((bf16[16,48,96]{2,0,1:T(8,128)(2,1)}), bf16[16,48,96]{2,0,1:T(8,128)(2,1)S(1)}, u32[]{:S(2)}, u32[]{:S(2)}) %all-to-all-start) | async-done | bytes 147488 | tf_op jit(solution)/shard_map/all_to_all | solution.py:69
  97.4 86.3 %while.16 = (s32[]{:T(128)}, f32[1536,48]{0,1:T(8,128)}, s32[]{:T(128)}, s32[768]{0:T(1024)S(1)}, f32[42,768]{1,0:T(8,128)S(1)}, /*index=5*/f32[42,768]{1,0:T(8,...) while((s32[]{:T(128)}, f32[1536,48]{0,1:T(8,128)}, ...), condition=%wide.region_1.2_spmd.clone.clone.clone, body=%wide.region_0.1_spmd.clone.clone.clone.sunk | while | flops 244571136 | bytes 22636492 | solution.py:97
  97.4 5.3 %fusion.49 = (f32[128,768]{1,0:T(8,128)S(1)}, f32[128,768]{1,0:T(8,128)S(1)}) fusion(f32[]{:T(128)} %get-tuple-element.544, pred[]{:T(512)} %get-tuple-element.541, s32[]{:T(128)} %get-tuple-element.543, s32[768]{0:T(1024)S(1)} %get-tuple-element.537, s32[128]{0:T(128)S(1)} %get-tuple-element.542), kind=kLoop, calls=%fused_computation.22.clone.1 | loop fusion | flops 1081344 | bytes 790025 | tf_op jit(solution)/shard_map/cos | solution.py:16
  104.7 1.0 copy-done
  107.1 2.6 convolution_add_fusion.2
  109.7 5.3 %fusion.49 = (f32[128,768]{1,0:T(8,128)S(1)}, f32[128,768]{1,0:T(8,128)S(1)}) fusion(f32[]{:T(128)} %get-tuple-element.544, pred[]{:T(512)} %get-tuple-element.541, s32[]{:T(128)} %get-tuple-element.543, s32[768]{0:T(1024)S(1)} %get-tuple-element.537, s32[128]{0:T(128)S(1)} %get-tuple-element.542), kind=kLoop, calls=%fused_computation.22.clone.1 | loop fusion | flops 1081344 | bytes 790025 | tf_op jit(solution)/shard_map/cos | solution.py:16
  119.4 2.6 convolution_add_fusion.2
  122.1 5.3 %fusion.49 = (f32[128,768]{1,0:T(8,128)S(1)}, f32[128,768]{1,0:T(8,128)S(1)}) fusion(f32[]{:T(128)} %get-tuple-element.544, pred[]{:T(512)} %get-tuple-element.541, s32[]{:T(128)} %get-tuple-element.543, s32[768]{0:T(1024)S(1)} %get-tuple-element.537, s32[128]{0:T(128)S(1)} %get-tuple-element.542), kind=kLoop, calls=%fused_computation.22.clone.1 | loop fusion | flops 1081344 | bytes 790025 | tf_op jit(solution)/shard_map/cos | solution.py:16
  129.3 1.0 copy-done
  131.7 2.6 convolution_add_fusion.2
  134.4 5.3 %fusion.49 = (f32[128,768]{1,0:T(8,128)S(1)}, f32[128,768]{1,0:T(8,128)S(1)}) fusion(f32[]{:T(128)} %get-tuple-element.544, pred[]{:T(512)} %get-tuple-element.541, s32[]{:T(128)} %get-tuple-element.543, s32[768]{0:T(1024)S(1)} %get-tuple-element.537, s32[128]{0:T(128)S(1)} %get-tuple-element.542), kind=kLoop, calls=%fused_computation.22.clone.1 | loop fusion | flops 1081344 | bytes 790025 | tf_op jit(solution)/shard_map/cos | solution.py:16
  144.1 2.6 convolution_add_fusion.2
  146.7 5.3 %fusion.49 = (f32[128,768]{1,0:T(8,128)S(1)}, f32[128,768]{1,0:T(8,128)S(1)}) fusion(f32[]{:T(128)} %get-tuple-element.544, pred[]{:T(512)} %get-tuple-element.541, s32[]{:T(128)} %get-tuple-element.543, s32[768]{0:T(1024)S(1)} %get-tuple-element.537, s32[128]{0:T(128)S(1)} %get-tuple-element.542), kind=kLoop, calls=%fused_computation.22.clone.1 | loop fusion | flops 1081344 | bytes 790025 | tf_op jit(solution)/shard_map/cos | solution.py:16
  154.0 1.0 copy-done
  156.4 2.6 convolution_add_fusion.2
  159.1 5.3 %fusion.49 = (f32[128,768]{1,0:T(8,128)S(1)}, f32[128,768]{1,0:T(8,128)S(1)}) fusion(f32[]{:T(128)} %get-tuple-element.544, pred[]{:T(512)} %get-tuple-element.541, s32[]{:T(128)} %get-tuple-element.543, s32[768]{0:T(1024)S(1)} %get-tuple-element.537, s32[128]{0:T(128)S(1)} %get-tuple-element.542), kind=kLoop, calls=%fused_computation.22.clone.1 | loop fusion | flops 1081344 | bytes 790025 | tf_op jit(solution)/shard_map/cos | solution.py:16
  168.7 2.6 convolution_add_fusion.2
  171.4 5.3 %fusion.49 = (f32[128,768]{1,0:T(8,128)S(1)}, f32[128,768]{1,0:T(8,128)S(1)}) fusion(f32[]{:T(128)} %get-tuple-element.544, pred[]{:T(512)} %get-tuple-element.541, s32[]{:T(128)} %get-tuple-element.543, s32[768]{0:T(1024)S(1)} %get-tuple-element.537, s32[128]{0:T(128)S(1)} %get-tuple-element.542), kind=kLoop, calls=%fused_computation.22.clone.1 | loop fusion | flops 1081344 | bytes 790025 | tf_op jit(solution)/shard_map/cos | solution.py:16
  181.1 2.6 convolution_add_fusion.2
  186.6 17.8 %all_to_all.30 = bf16[48,2,768]{2,1,0:T(2,128)(2,1)S(1)} all-to-all(bf16[48,2,768]{2,1,0:T(2,128)(2,1)S(1)} %reshape.186), channel_id=1, replica_groups=mesh['wave'=48,'lev'=16] {'wave'}, dimensions={0} | all-to-all | bytes 294912 | tf_op jit(solution)/shard_map/all_to_all | solution.py:102
  205.6 2.4 copy.57
  208.0 56.5 %reduce-scatter.2.cloned.1.call-done = bf16[6,8,1280]{2,1,0:T(8,128)(2,1)} async-done(((bf16[96,8,1280]{2,1,0:T(8,128)(2,1)}), bf16[6,8,1280]{2,1,0:T(8,128)(2,1)}) %reduce-scatter.2.cloned.1.call-update) | async-done | bytes 122896 | tf_op jit(solution)/shard_map/reduce_scatter | solution.py:107
  266.7 1.1 reshape.179
  (221 shorter events, 40.2 us)
Async XLA Ops:
  6.5 57.5 %all-gather.2.cloned.1.call-start = ((), (), s32[]{:S(2)}) async-start(), calls=%async_computation.3 | async-start | bytes 2088960 | tf_op jit(solution)/shard_map/all_gather | solution.py:64
  15.8 48.3 %copy-start.3 = (bf16[8,1,48,1280]{3,2,1,0:T(8,128)(2,1)}, bf16[8,1,48,1280]{3,2,1,0:T(8,128)(2,1)S(1)}, u32[]{:S(2)}) copy-start(bf16[8,1,48,1280]{3,2,1,0:T(8,128)(2,1)S(1)} %get-tuple-element.395) | copy-start | bytes 2949124
  19.9 46.4 %copy-start.1 = (bf16[8,1,48,1280]{3,2,1,0:T(8,128)(2,1)}, bf16[8,1,48,1280]{3,2,1,0:T(8,128)(2,1)S(1)}, u32[]{:S(2)}) copy-start(bf16[8,1,48,1280]{3,2,1,0:T(8,128)(2,1)S(1)} %broadcast_select_fusion) | copy-start | bytes 2949124
  64.0 16.3 %copy-start.5 = (s32[768]{0:T(1024)S(1)}, s32[768]{0:T(1024)}, u32[]{:S(2)}) copy-start(s32[768]{0:T(1024)} %param.11) | copy-start | bytes 9220
  67.0 27.4 %all-to-all-start = ((bf16[16,48,96]{2,0,1:T(8,128)(2,1)}), bf16[16,48,96]{2,0,1:T(8,128)(2,1)S(1)}, u32[]{:S(2)}, u32[]{:S(2)}) async-start(bf16[16,48,96]{2,0,1:T(8,128)(2,1)} %copy.51), calls=%async_computation | async-start | bytes 393216 | tf_op jit(solution)/shard_map/all_to_all | solution.py:69
  80.0 184.5 %reduce-scatter.2.cloned.1.call-start = ((), (), s32[]{:S(2)}) async-start(), calls=%async_computation.4 | async-start | bytes 2088960 | tf_op jit(solution)/shard_map/reduce_scatter | solution.py:107
  97.4 5.3 %copy-start.6 = (f32[42,768]{1,0:T(8,128)}, f32[42,768]{1,0:T(8,128)S(1)}, u32[]{:S(2)}) copy-start(f32[42,768]{1,0:T(8,128)S(1)} %get-tuple-element.539) | copy-start | bytes 387076 | tf_op jit(solution)/shard_map/while
  97.4 5.3 %copy-start.8 = (f32[42,768]{1,0:T(8,128)}, f32[42,768]{1,0:T(8,128)S(1)}, u32[]{:S(2)}) copy-start(f32[42,768]{1,0:T(8,128)S(1)} %get-tuple-element.538) | copy-start | bytes 387076 | tf_op jit(solution)/shard_map/while
  97.4 5.3 %copy-start.11 = (s32[128]{0:T(128)}, s32[128]{0:T(128)S(1)}, u32[]{:S(2)}) copy-start(s32[128]{0:T(128)S(1)} %get-tuple-element.542) | copy-start | bytes 1540 | tf_op jit(solution)/shard_map/while
  109.7 5.3 %copy-start.6 = (f32[42,768]{1,0:T(8,128)}, f32[42,768]{1,0:T(8,128)S(1)}, u32[]{:S(2)}) copy-start(f32[42,768]{1,0:T(8,128)S(1)} %get-tuple-element.539) | copy-start | bytes 387076 | tf_op jit(solution)/shard_map/while
  109.7 5.3 %copy-start.8 = (f32[42,768]{1,0:T(8,128)}, f32[42,768]{1,0:T(8,128)S(1)}, u32[]{:S(2)}) copy-start(f32[42,768]{1,0:T(8,128)S(1)} %get-tuple-element.538) | copy-start | bytes 387076 | tf_op jit(solution)/shard_map/while
  109.7 5.3 %copy-start.11 = (s32[128]{0:T(128)}, s32[128]{0:T(128)S(1)}, u32[]{:S(2)}) copy-start(s32[128]{0:T(128)S(1)} %get-tuple-element.542) | copy-start | bytes 1540 | tf_op jit(solution)/shard_map/while
  119.4 2.6 copy-start.7
  122.0 5.3 %copy-start.6 = (f32[42,768]{1,0:T(8,128)}, f32[42,768]{1,0:T(8,128)S(1)}, u32[]{:S(2)}) copy-start(f32[42,768]{1,0:T(8,128)S(1)} %get-tuple-element.539) | copy-start | bytes 387076 | tf_op jit(solution)/shard_map/while
  122.0 5.3 %copy-start.8 = (f32[42,768]{1,0:T(8,128)}, f32[42,768]{1,0:T(8,128)S(1)}, u32[]{:S(2)}) copy-start(f32[42,768]{1,0:T(8,128)S(1)} %get-tuple-element.538) | copy-start | bytes 387076 | tf_op jit(solution)/shard_map/while
  122.0 5.3 %copy-start.11 = (s32[128]{0:T(128)}, s32[128]{0:T(128)S(1)}, u32[]{:S(2)}) copy-start(s32[128]{0:T(128)S(1)} %get-tuple-element.542) | copy-start | bytes 1540 | tf_op jit(solution)/shard_map/while
  134.3 5.3 %copy-start.6 = (f32[42,768]{1,0:T(8,128)}, f32[42,768]{1,0:T(8,128)S(1)}, u32[]{:S(2)}) copy-start(f32[42,768]{1,0:T(8,128)S(1)} %get-tuple-element.539) | copy-start | bytes 387076 | tf_op jit(solution)/shard_map/while
  134.4 5.3 %copy-start.8 = (f32[42,768]{1,0:T(8,128)}, f32[42,768]{1,0:T(8,128)S(1)}, u32[]{:S(2)}) copy-start(f32[42,768]{1,0:T(8,128)S(1)} %get-tuple-element.538) | copy-start | bytes 387076 | tf_op jit(solution)/shard_map/while
  134.4 5.3 %copy-start.11 = (s32[128]{0:T(128)}, s32[128]{0:T(128)S(1)}, u32[]{:S(2)}) copy-start(s32[128]{0:T(128)S(1)} %get-tuple-element.542) | copy-start | bytes 1540 | tf_op jit(solution)/shard_map/while
  144.0 2.6 copy-start.7
  146.7 5.3 %copy-start.6 = (f32[42,768]{1,0:T(8,128)}, f32[42,768]{1,0:T(8,128)S(1)}, u32[]{:S(2)}) copy-start(f32[42,768]{1,0:T(8,128)S(1)} %get-tuple-element.539) | copy-start | bytes 387076 | tf_op jit(solution)/shard_map/while
  146.7 5.3 %copy-start.8 = (f32[42,768]{1,0:T(8,128)}, f32[42,768]{1,0:T(8,128)S(1)}, u32[]{:S(2)}) copy-start(f32[42,768]{1,0:T(8,128)S(1)} %get-tuple-element.538) | copy-start | bytes 387076 | tf_op jit(solution)/shard_map/while
  146.7 5.3 %copy-start.11 = (s32[128]{0:T(128)}, s32[128]{0:T(128)S(1)}, u32[]{:S(2)}) copy-start(s32[128]{0:T(128)S(1)} %get-tuple-element.542) | copy-start | bytes 1540 | tf_op jit(solution)/shard_map/while
  159.0 5.3 %copy-start.6 = (f32[42,768]{1,0:T(8,128)}, f32[42,768]{1,0:T(8,128)S(1)}, u32[]{:S(2)}) copy-start(f32[42,768]{1,0:T(8,128)S(1)} %get-tuple-element.539) | copy-start | bytes 387076 | tf_op jit(solution)/shard_map/while
  159.0 5.3 %copy-start.8 = (f32[42,768]{1,0:T(8,128)}, f32[42,768]{1,0:T(8,128)S(1)}, u32[]{:S(2)}) copy-start(f32[42,768]{1,0:T(8,128)S(1)} %get-tuple-element.538) | copy-start | bytes 387076 | tf_op jit(solution)/shard_map/while
  159.0 5.3 %copy-start.11 = (s32[128]{0:T(128)}, s32[128]{0:T(128)S(1)}, u32[]{:S(2)}) copy-start(s32[128]{0:T(128)S(1)} %get-tuple-element.542) | copy-start | bytes 1540 | tf_op jit(solution)/shard_map/while
  168.7 2.6 copy-start.7
  171.4 5.3 %copy-start.6 = (f32[42,768]{1,0:T(8,128)}, f32[42,768]{1,0:T(8,128)S(1)}, u32[]{:S(2)}) copy-start(f32[42,768]{1,0:T(8,128)S(1)} %get-tuple-element.539) | copy-start | bytes 387076 | tf_op jit(solution)/shard_map/while
  171.4 5.3 %copy-start.8 = (f32[42,768]{1,0:T(8,128)}, f32[42,768]{1,0:T(8,128)S(1)}, u32[]{:S(2)}) copy-start(f32[42,768]{1,0:T(8,128)S(1)} %get-tuple-element.538) | copy-start | bytes 387076 | tf_op jit(solution)/shard_map/while
  171.4 5.3 %copy-start.11 = (s32[128]{0:T(128)}, s32[128]{0:T(128)S(1)}, u32[]{:S(2)}) copy-start(s32[128]{0:T(128)S(1)} %get-tuple-element.542) | copy-start | bytes 1540 | tf_op jit(solution)/shard_map/while
  184.7 20.2 %copy-start.2 = (bf16[8,1,48,1280]{3,2,1,0:T(8,128)(2,1)S(1)}, bf16[8,1,48,1280]{3,2,1,0:T(8,128)(2,1)}, u32[]{:S(2)}) copy-start(bf16[8,1,48,1280]{3,2,1,0:T(8,128)(2,1)} %copy-done.1) | copy-start | bytes 2949124
  184.7 20.2 %copy-start.4 = (bf16[8,1,48,1280]{3,2,1,0:T(8,128)(2,1)S(1)}, bf16[8,1,48,1280]{3,2,1,0:T(8,128)(2,1)}, u32[]{:S(2)}) copy-start(bf16[8,1,48,1280]{3,2,1,0:T(8,128)(2,1)} %copy-done.3) | copy-start | bytes 2949124
  (32 other events, 66.3 us)
Sparse Core Ops, SparseCore 0:
  11.6 52.3 all-gather.1
  208.1 56.3 reduce-scatter.1

commit v2 on v1

--- a/solution.py
+++ b/solution.py
@@ -16,7 +16,7 @@
     return (jnp.cos(angle), jnp.sin(angle))
 
 
-def compose_table(count, waves, coarse_cos, coarse_sin, fine_cos, fine_sin, lon_rows):
+def compose_table(row_limit, count, waves, coarse_cos, coarse_sin, fine_cos, fine_sin, lon_rows):
     cosine = (
         coarse_cos[:, None, :] * fine_cos[None, :, :]
         - coarse_sin[:, None, :] * fine_sin[None, :, :]
@@ -28,7 +28,7 @@
     rows_total = lon_rows.shape[0]
     cosine = cosine.reshape(rows_total, waves.shape[0])
     sine = sine.reshape(rows_total, waves.shape[0])
-    usable = (lon_rows[:, None] < count) & (2 * waves[None, :] < count)
+    usable = (lon_rows[:, None] < row_limit) & (2 * waves[None, :] < count)
     cosine = jnp.where(usable, cosine, jnp.zeros((), jnp.float32))
     sine = jnp.where(usable, -sine, jnp.zeros((), jnp.float32))
     return jnp.concatenate([cosine, sine], axis=1).astype(jnp.bfloat16)
@@ -69,34 +69,44 @@
     fourier = lax.all_to_all(four_local, "wave", split_axis=1, concat_axis=0, tiled=True)
     mine = fourier.shape[1]
     half_cols = columns // 2
-    fine_rows = lax.iota(jnp.int32, 128)
-    coarse_rows = lax.iota(jnp.int32, NLONPAD // 128) * 128
-    coarse_step = LON_BLOCK // 128
     lat_index = lev_index * lat_band + wave_index * mine + 0
     count = lax.dynamic_slice_in_dim(nlon, lat_index, 1)[0]
     weight = lax.dynamic_slice_in_dim(weights, lat_index, 1)[0]
+    half_rows = NLONPAD // 2
+    half = count // 2
+    fine_rows = lax.iota(jnp.int32, 128)
+    coarse_rows = lax.iota(jnp.int32, half_rows // 128) * 128
+    lon_rows = lax.iota(jnp.int32, half_rows)
+    fine_cos, fine_sin = angle_parts(count, assignment, fine_rows)
+    coarse_cos, coarse_sin = angle_parts(count, assignment, coarse_rows)
+    table = compose_table(
+        half + 1, count, assignment, coarse_cos, coarse_sin, fine_cos, fine_sin, lon_rows
+    )
     pairs = fourier[:, 0, :].reshape(all_slots, half_cols, 2)
-    stacked = jnp.concatenate([pairs[:, :, 0], pairs[:, :, 1]], axis=0)
-    fine_cos, fine_sin = angle_parts(count, assignment, fine_rows)
-    coarse_cos_all, coarse_sin_all = angle_parts(count, assignment, coarse_rows)
-
-    def lon_block(block_step, total):
-        lon_rows = block_step * LON_BLOCK + lax.iota(jnp.int32, LON_BLOCK)
-        coarse_cos = lax.dynamic_slice_in_dim(coarse_cos_all, block_step * coarse_step, coarse_step)
-        coarse_sin = lax.dynamic_slice_in_dim(coarse_sin_all, block_step * coarse_step, coarse_step)
-        table = compose_table(
-            count, assignment, coarse_cos, coarse_sin, fine_cos, fine_sin, lon_rows
-        )
-        grid = 2.0 * jnp.dot(table, stacked, preferred_element_type=jnp.float32)
-        products = quadratic(grid)
-        return total + lax.dot_general(
-            table, products, (((0,), (0,)), ((), ())), preferred_element_type=jnp.float32
-        )
-
-    start_total = jnp.zeros((2 * all_slots, half_cols), jnp.float32)
-    total = lax.fori_loop(0, NLONPAD // LON_BLOCK, lon_block, start_total)
-    back = total * (weight / count.astype(jnp.float32))
-    joined = jnp.stack([back[:all_slots], back[all_slots:]], axis=-1).reshape(all_slots, columns)
+    zero_bf = jnp.zeros((), jnp.bfloat16)
+    blank = jnp.zeros((all_slots, half_cols), jnp.bfloat16)
+    split = jnp.concatenate(
+        [
+            jnp.concatenate([pairs[:, :, 0], blank], axis=1),
+            jnp.concatenate([blank, pairs[:, :, 1]], axis=1),
+        ],
+        axis=0,
+    )
+    parts = jnp.dot(table, split, preferred_element_type=jnp.float32)
+    even, odd = parts[:, :half_cols], parts[:, half_cols:]
+    grid_pos = 2.0 * (even + odd)
+    grid_neg = 2.0 * (even - odd)
+    mirrored = (lon_rows > 0) & (lon_rows < half)
+    prod_pos = quadratic(grid_pos)
+    prod_neg = jnp.where(mirrored[:, None], quadratic(grid_neg), zero_bf)
+    both = jnp.concatenate([prod_pos, prod_neg], axis=1)
+    total = lax.dot_general(
+        table, both, (((0,), (0,)), ((), ())), preferred_element_type=jnp.float32
+    )
+    real = total[:all_slots, :half_cols] + total[:all_slots, half_cols:]
+    imag = total[all_slots:, :half_cols] - total[all_slots:, half_cols:]
+    scale = weight / count.astype(jnp.float32)
+    joined = jnp.stack([real * scale, imag * scale], axis=-1).reshape(all_slots, columns)
     analysed_rows = [joined.astype(jnp.bfloat16)]
     analysed = jnp.stack(analysed_rows, axis=1)
     returned = lax.all_to_all(analysed, "wave", split_axis=0, concat_axis=1, tiled=True)

time: 276 us -> 201 us (0.73)
  other arithmetic: 60.3 us -> 26.3 us
  waiting for transfers between devices: 113 us -> 92.2 us
  matrix products: 26.9 us -> 12.6 us
  local copies, waits for them, and re-layouts: 26.4 us -> 17.9 us
  between operations: 16.2 us -> 19.2 us
    cos x7 -> x2, other arithmetic: 36.9 us -> 6.37 us  [angle_parts(): return (jnp.cos(angle), jnp.sin(angle))]
    dot_general x14 -> x2, matrix products: 23.9 us -> 9.67 us  [the longest x1 5.25 us: per_device(): parts = jnp.dot(table, split, preferred_element_type=jnp.float32)]
    all_gather x1, waiting for transfers between devices: 44.2 us -> 30.2 us  [per_device(): spec_all = lax.all_gather(packed_spec, 'lev', axis=0, tiled=True)]
    while x112 -> x0, local copies, waits for them, and re-layouts: 7.54 us -> none
    all_to_all x1, waiting for transfers between devices: 12 us -> 5.54 us  [per_device(): lax.all_to_all(four_local, 'wave', split_axis=1, concat_axis=0, tiled=True)]
    lt x7 -> x2, other arithmetic: 4.46 us -> 0.69 us  [compose_table(): usable = (lon_rows[:, None] < row_limit) & (2 * waves[None, :] < count)]
    another operation x16 -> x5, other arithmetic: 6.22 us -> 7.6 us
  transfers between devices with their start and end apart: 3 -> 3, of which waited for: 3 -> 3; matrix products, arithmetic and copies ran while one was open for 3% -> 13% of each run, Pallas kernels for 0% -> 0%
where the time goes in v2:
time: 201 us; the launch traced here: 200 us
  waiting for transfers between devices  92.2 us (46%)
  other arithmetic  26.3 us (13%)
  between operations  19.2 us (10%)
  blocking collectives  18.6 us (9%)
  local copies, waits for them, and re-layouts  17.9 us (9%)
  starting transfers between devices  13.2 us (7%)
  matrix products  12.6 us (6%)
    reduce_scatter x1, waiting for transfers between devices, per_device(): lax.psum_scatter(band_term.astype(jnp.bfloat16), 'lev', scatter_dimension...  56.5 us
    all_gather x1, waiting for transfers between devices, per_device(): spec_all = lax.all_gather(packed_spec, 'lev', axis=0, tiled=True)  30.2 us
    all_to_all x1, blocking collectives, per_device(): lax.all_to_all(analysed, 'wave', split_axis=0, concat_axis=1, tiled=True)  18.6 us
    all_to_all x1, starting transfers between devices, per_device(): lax.all_to_all(four_local, 'wave', split_axis=1, concat_axis=0, tiled=True)  13 us
    another operation x3, other arithmetic  7.54 us
    cos x2, other arithmetic, angle_parts(): return (jnp.cos(angle), jnp.sin(angle))  6.37 us
    all_to_all x1, waiting for transfers between devices, per_device(): lax.all_to_all(four_local, 'wave', split_axis=1, concat_axis=0, tiled=True)  5.54 us
    dot_general x1, matrix products, per_device(): parts = jnp.dot(table, split, preferred_element_type=jnp.float32)  5.25 us
  transfers between devices with their start and end apart: 3, of which 3 were waited for; matrix products, arithmetic and copies ran while one was open for 13% of the time, Pallas kernels for 0%

profile of v2, /device:TPU:1, one launch (start us, length us, event | category | flops | bytes accessed | tf_op | source)
XLA Modules:
  0.0 200.0 jit_solution(10884744803289183241)
XLA Ops:
  6.5 0.8 dynamic_slice.9
  7.6 1.0 reshape.267
  9.0 1.8 rev.10
  10.8 0.7 bitcast_select_fusion
  11.5 1.3 dynamic_slice.10
  17.7 2.6 %slice_select_fusion = (bf16[8,1,48,1280]{3,2,1,0:T(8,128)(2,1)}, bf16[8,1,48,1280]{3,2,1,0:T(8,128)(2,1)S(1)}) fusion(bf16[8,2,48,1280]{3,2,1,0:T(8,128)(2,1)} %bitcast.53, pred[8,1280]{1,0:T(8,128)(4,1)S(1)} %iota_compare_fusion.2), kind=kLoop, calls=%fused_computation.15 | loop fusion | flops 491520 | bytes 3942400 | tf_op jit(solution)/shard_map/jit(_where)/select_n | solution.py:59
  20.3 1.4 rev.9
  21.9 0.7 multiply_compare_fusion
  22.6 1.1 fusion.46
  23.7 5.3 %fusion.30 = (f32[128,768]{1,0:T(8,128)S(1)}, f32[128,768]{1,0:T(8,128)S(1)}) fusion(f32[]{:T(128)S(6)} %convert_element_type.58, pred[]{:T(512)S(6)} %lt.119, s32[]{:T(128)S(6)} %select_n.100, s32[768]{0:T(1024)S(1)} %copy-done.2, s32[128]{0:T(128)S(1)} %and_select_fusion.2), kind=kLoop, calls=%fused_computation.47 | loop fusion | flops 1081344 | bytes 790025 | tf_op jit(solution)/shard_map/cos | solution.py:16
  29.1 4.8 %multiply_subtract_fusion = (bf16[21,128,768]{2,1,0:T(8,128)(2,1)}, bf16[21,128,768]{2,1,0:T(8,128)(2,1)}) fusion(f32[128,768]{1,0:T(8,128)S(1)} %get-tuple-element.28, f32[21,768]{1,0:T(8,128)S(1)} %get-tuple-element.26, f32[128,768]{1,0:T(8,128)S(1)} %get-tuple-element.27, f32[21,768]{1,0:T(8,128)S(1)} %get-tuple-element.25), kind=kLoop, calls=%fused_computation.6 | loop fusion | flops 18579456 | bytes 9172992 | tf_op jit(solution)/shard_map/sub | solution.py:21
  33.9 30.2 %all-gather.2.cloned.1.call-done = bf16[96,8,1280]{2,1,0:T(8,128)(2,1)} async-done(((bf16[6,8,1280]{2,1,0:T(8,128)(2,1)}), bf16[96,8,1280]{2,1,0:T(8,128)(2,1)}) %all-gather.2.cloned.1.call-update) | async-done | bytes 1966096 | tf_op jit(solution)/shard_map/all_gather | solution.py:64
  64.0 2.2 %fusion.7 = bf16[8,2,48,96]{3,2,1,0:T(8,128)(2,1)S(1)} fusion(bf16[96,8,1280,1]{2,1,0,3:T(8,128)(2,1)} %bitcast.59, bf16[8,1,48,1280]{3,2,1,0:T(8,128)(2,1)S(1)} %broadcast_select_fusion, bf16[8,1,48,1280]{3,2,1,0:T(8,128)(2,1)S(1)} %copy-done), kind=kOutput, calls=%fused_computation.14 | convolution fusion | flops 189800448 | bytes 4079616 | tf_op jit(solution)/shard_map/pxlk,cpk->pxlc/dot_general | solution.py:66
  66.3 0.7 copy.39
  67.0 13.0 %all-to-all-start = ((bf16[16,48,96]{2,0,1:T(8,128)(2,1)}), bf16[16,48,96]{2,0,1:T(8,128)(2,1)S(1)}, u32[]{:S(2)}, u32[]{:S(2)}) async-start(bf16[16,48,96]{2,0,1:T(8,128)(2,1)} %copy.39), calls=%async_computation | async-start | bytes 393216 | tf_op jit(solution)/shard_map/all_to_all | solution.py:69
  80.2 6.6 %fusion = (bf16[2688,768]{1,0:T(8,128)(2,1)}, bf16[2688,768]{1,0:T(8,128)(2,1)}) fusion(bf16[21,128,768]{2,1,0:T(8,128)(2,1)} %get-tuple-element.9, pred[768]{0:T(1024)(128)(4,1)S(1)} %multiply_compare_fusion, pred[2688]{0:T(1024)(128)(4,1)S(1)} %iota_compare_fusion.5, bf16[21,128,768]{2,1,0:T(8,128)(2,1)} %get-tuple-element.10), kind=kLoop, calls=%fused_computation.2 | loop fusion | flops 6193152 | bytes 16518528 | tf_op jit(solution)/shard_map/convert.10
  86.8 1.3 dynamic_slice.11
  88.9 5.5 %all-to-all-done = bf16[16,48,96]{2,0,1:T(8,128)(2,1)S(1)} async-done(((bf16[16,48,96]{2,0,1:T(8,128)(2,1)}), bf16[16,48,96]{2,0,1:T(8,128)(2,1)S(1)}, u32[]{:S(2)}, u32[]{:S(2)}) %all-to-all-start) | async-done | bytes 147488 | tf_op jit(solution)/shard_map/all_to_all | solution.py:69
  94.4 0.9 copy.40
  95.3 0.9 reshape_squeeze.3
  96.4 5.3 %fusion.3 = f32[2688,96]{0,1:T(8,128)S(1)} fusion(bf16[2688,768]{1,0:T(8,128)(2,1)} %get-tuple-element.30, bf16[2688,768]{1,0:T(8,128)(2,1)} %get-tuple-element.29, bf16[768,48]{0,1:T(8,128)(2,1)S(1)} %get-tuple-element.31, bf16[768,48]{0,1:T(8,128)(2,1)S(1)} %get-tuple-element.32), kind=kOutput, calls=%fused_computation.8 | convolution fusion | flops 810418176 | bytes 9437184 | tf_op jit(solution)/shard_map/dot_general | solution.py:95
  102.5 0.6 pad_maximum_fusion.9
  104.0 0.6 pad_maximum_fusion.10
  104.9 4.4 %fusion.2 = f32[1536,96]{0,1:T(8,128)S(1)} fusion(bf16[2688,768]{1,0:T(8,128)(2,1)} %get-tuple-element.30, bf16[2688,768]{1,0:T(8,128)(2,1)} %get-tuple-element.29, bf16[2688,48]{0,1:T(8,128)(2,1)S(1)} %broadcast_select_fusion.1, bf16[2688,48]{0,1:T(8,128)(2,1)S(1)} %convert_element_type.61), kind=kOutput, calls=%fused_computation.7 | convolution fusion | flops 810270720 | bytes 9363456 | tf_op jit(solution)/shard_map/dot_general | solution.py:103
  110.1 0.7 reduce.2
  111.3 18.6 %all_to_all.30 = bf16[48,2,768]{2,1,0:T(2,128)(2,1)S(1)} all-to-all(bf16[48,2,768]{2,1,0:T(2,128)(2,1)S(1)} %reshape.276), channel_id=1, replica_groups=mesh['wave'=48,'lev'=16] {'wave'}, dimensions={0} | all-to-all | bytes 294912 | tf_op jit(solution)/shard_map/all_to_all | solution.py:112
  130.3 0.7 fusion.4
  131.0 2.4 %copy.44 = bf16[96,8,1280]{2,1,0:T(8,128)(2,1)} copy(bf16[96,8,1280]{2,0,1:T(8,128)(2,1)S(1)} %fusion.4) | data formatting | bytes 3932160 | tf_op jit(solution)/shard_map/convert_element_type | solution.py:118
  133.4 56.5 %reduce-scatter.2.cloned.1.call-done = bf16[6,8,1280]{2,1,0:T(8,128)(2,1)} async-done(((bf16[96,8,1280]{2,1,0:T(8,128)(2,1)}), bf16[6,8,1280]{2,1,0:T(8,128)(2,1)}) %reduce-scatter.2.cloned.1.call-update) | async-done | bytes 122896 | tf_op jit(solution)/shard_map/reduce_scatter | solution.py:117
  189.9 0.9 fusion.28
  190.8 0.8 rev.11
  192.0 1.1 reshape.272
  (41 shorter events, 5.4 us)
Async XLA Ops:
  6.5 57.5 %all-gather.2.cloned.1.call-start = ((), (), s32[]{:S(2)}) async-start(), calls=%async_computation.3 | async-start | bytes 2088960 | tf_op jit(solution)/shard_map/all_gather | solution.py:64
  8.6 13.3 %copy-start.2 = (s32[768]{0:T(1024)S(1)}, s32[768]{0:T(1024)}, u32[]{:S(2)}) copy-start(s32[768]{0:T(1024)} %param.9) | copy-start | bytes 9220
  29.1 35.0 %copy-start = (bf16[8,1,48,1280]{3,2,1,0:T(8,128)(2,1)S(1)}, bf16[8,1,48,1280]{3,2,1,0:T(8,128)(2,1)}, u32[]{:S(2)}) copy-start(bf16[8,1,48,1280]{3,2,1,0:T(8,128)(2,1)} %get-tuple-element.5) | copy-start | bytes 2949124
  67.0 27.4 %all-to-all-start = ((bf16[16,48,96]{2,0,1:T(8,128)(2,1)}), bf16[16,48,96]{2,0,1:T(8,128)(2,1)S(1)}, u32[]{:S(2)}, u32[]{:S(2)}) async-start(bf16[16,48,96]{2,0,1:T(8,128)(2,1)} %copy.39), calls=%async_computation | async-start | bytes 393216 | tf_op jit(solution)/shard_map/all_to_all | solution.py:69
  80.0 109.9 %reduce-scatter.2.cloned.1.call-start = ((), (), s32[]{:S(2)}) async-start(), calls=%async_computation.4 | async-start | bytes 2088960 | tf_op jit(solution)/shard_map/reduce_scatter | solution.py:117
  109.4 20.9 %copy-start.1 = (bf16[8,1,48,1280]{3,2,1,0:T(8,128)(2,1)S(1)}, bf16[8,1,48,1280]{3,2,1,0:T(8,128)(2,1)}, u32[]{:S(2)}) copy-start(bf16[8,1,48,1280]{3,2,1,0:T(8,128)(2,1)} %get-tuple-element.5) | copy-start | bytes 2949124
Sparse Core Ops, SparseCore 0:
  11.7 52.3 all-gather.1
  133.5 56.3 reduce-scatter.1

commit v3 on v2

--- a/solution.py
+++ b/solution.py
@@ -114,11 +114,13 @@
     band_term = jnp.einsum(
         "pxlc,pxlk->cpk", returned, packed_leg, preferred_element_type=jnp.float32
     )
-    summed = lax.psum_scatter(
-        band_term.astype(jnp.bfloat16), "lev", scatter_dimension=0, tiled=True
+    lev_count = lax.axis_size("lev")
+    shares = band_term.astype(jnp.bfloat16).reshape(
+        lev_count, columns // lev_count, pairs_n, kmax_width
     )
+    gathered = lax.all_to_all(shares, "lev", split_axis=0, concat_axis=0, tiled=True)
+    summed = jnp.sum(gathered.astype(jnp.float32), axis=0)
     zero_f = jnp.zeros((), jnp.float32)
-    summed = summed.astype(jnp.float32)
     out_a = jnp.where(front[None], summed, zero_f)
     out_b = jnp.where(front[None], zero_f, summed)[:, :, ::-1]
     out = jnp.stack([out_a, out_b], axis=2)

time: 201 us -> 196 us (0.975)
  waiting for transfers between devices: 92.2 us -> 36.6 us
  blocking collectives: 18.6 us -> 73.5 us
  local copies, waits for them, and re-layouts: 17.9 us -> 15.5 us
    reduce_scatter x1 -> x0, waiting for transfers between devices: 56.5 us -> none  [per_device(): lax.psum_scatter(band_term.astype(jnp.bfloat16), 'lev', scatter_dimension...]
    all_to_all x0 -> x1, blocking collectives: none -> 55.4 us  [per_device(): lax.all_to_all(shares, 'lev', split_axis=0, concat_axis=0, tiled=True)]
  transfers between devices with their start and end apart: 3 -> 2, of which waited for: 3 -> 2; matrix products, arithmetic and copies ran while one was open for 13% -> 13% of each run, Pallas kernels for 0% -> 0%
where the time goes in v3:
time: 196 us
  blocking collectives  73.5 us (38%)
  waiting for transfers between devices  36.6 us (19%)
  other arithmetic  25.5 us (13%)
  between operations  18.7 us (10%)
  local copies, waits for them, and re-layouts  15.5 us (8%)
  starting transfers between devices  13.2 us (7%)
  matrix products  12.6 us (6%)
    all_to_all x1, blocking collectives, per_device(): lax.all_to_all(shares, 'lev', split_axis=0, concat_axis=0, tiled=True)  55.4 us
    all_gather x1, waiting for transfers between devices, per_device(): spec_all = lax.all_gather(packed_spec, 'lev', axis=0, tiled=True)  30.7 us
    all_to_all x1, blocking collectives, per_device(): lax.all_to_all(analysed, 'wave', split_axis=0, concat_axis=1, tiled=True)  18.1 us
    all_to_all x1, starting transfers between devices, per_device(): lax.all_to_all(four_local, 'wave', split_axis=1, concat_axis=0, tiled=True)  13.2 us
    another operation x3, other arithmetic  7.53 us
    cos x2, other arithmetic, angle_parts(): return (jnp.cos(angle), jnp.sin(angle))  6.37 us
    all_to_all x1, waiting for transfers between devices, per_device(): lax.all_to_all(four_local, 'wave', split_axis=1, concat_axis=0, tiled=True)  5.82 us
    dot_general x1, matrix products, per_device(): parts = jnp.dot(table, split, preferred_element_type=jnp.float32)  5.25 us
  transfers between devices with their start and end apart: 2, of which 2 were waited for; matrix products, arithmetic and copies ran while one was open for 13% of the time, Pallas kernels for 0%

profile of v3, /device:TPU:1, one launch (start us, length us, event | category | flops | bytes accessed | tf_op | source)
XLA Modules:
  0.0 195.6 jit_solution(11169890772082038725)
XLA Ops:
  6.5 0.8 dynamic_slice.9
  7.6 1.0 reshape.277
  9.0 0.9 rev.10
  9.9 0.7 fusion.35
  10.6 1.3 dynamic_slice.10
  16.3 2.6 %slice_select_fusion = (bf16[8,1,48,1280]{3,2,1,0:T(8,128)(2,1)}, bf16[8,1,48,1280]{3,2,1,0:T(8,128)(2,1)S(1)}) fusion(bf16[8,2,48,1280]{3,2,1,0:T(8,128)(2,1)} %bitcast.57, pred[8,1280]{1,0:T(8,128)(4,1)S(1)} %iota_compare_fusion.2), kind=kLoop, calls=%fused_computation.16 | loop fusion | flops 491520 | bytes 3942400 | tf_op jit(solution)/shard_map/jit(_where)/select_n | solution.py:59
  18.9 1.4 rev.9
  20.5 0.6 multiply_compare_fusion
  21.2 1.1 fusion.46
  22.3 5.3 %fusion.29 = (f32[128,768]{1,0:T(8,128)S(1)}, f32[128,768]{1,0:T(8,128)S(1)}) fusion(f32[]{:T(128)S(6)} %convert_element_type.58, pred[]{:T(512)S(6)} %lt.119, s32[]{:T(128)S(6)} %select_n.107, s32[768]{0:T(1024)S(1)} %copy-done.2, s32[128]{0:T(128)S(1)} %and_select_fusion.2), kind=kLoop, calls=%fused_computation.46 | loop fusion | flops 1081344 | bytes 790025 | tf_op jit(solution)/shard_map/cos | solution.py:16
  27.6 4.7 %multiply_subtract_fusion = (bf16[21,128,768]{2,1,0:T(8,128)(2,1)}, bf16[21,128,768]{2,1,0:T(8,128)(2,1)}) fusion(f32[128,768]{1,0:T(8,128)S(1)} %get-tuple-element.26, f32[21,768]{1,0:T(8,128)S(1)} %get-tuple-element.24, f32[128,768]{1,0:T(8,128)S(1)} %get-tuple-element.25, f32[21,768]{1,0:T(8,128)S(1)} %get-tuple-element.23), kind=kLoop, calls=%fused_computation.6 | loop fusion | flops 18579456 | bytes 9172992 | tf_op jit(solution)/shard_map/sub | solution.py:21
  32.4 30.7 %all-gather.2.cloned.1.call-done = bf16[96,8,1280]{2,1,0:T(8,128)(2,1)} async-done(((bf16[6,8,1280]{2,1,0:T(8,128)(2,1)}), bf16[96,8,1280]{2,1,0:T(8,128)(2,1)}) %all-gather.2.cloned.1.call-update) | async-done | bytes 1966096 | tf_op jit(solution)/shard_map/all_gather | solution.py:64
  63.1 2.2 %fusion.7 = bf16[8,2,48,96]{3,2,1,0:T(8,128)(2,1)S(1)} fusion(bf16[96,8,1280,1]{2,1,0,3:T(8,128)(2,1)} %bitcast.63, bf16[8,1,48,1280]{3,2,1,0:T(8,128)(2,1)S(1)} %broadcast_select_fusion, bf16[8,1,48,1280]{3,2,1,0:T(8,128)(2,1)S(1)} %copy-done), kind=kOutput, calls=%fused_computation.15 | convolution fusion | flops 189800448 | bytes 4079616 | tf_op jit(solution)/shard_map/pxlk,cpk->pxlc/dot_general | solution.py:66
  65.3 0.7 copy.26
  66.1 13.2 %all-to-all-start = ((bf16[16,48,96]{2,0,1:T(8,128)(2,1)}), bf16[16,48,96]{2,0,1:T(8,128)(2,1)S(1)}, u32[]{:S(2)}, u32[]{:S(2)}) async-start(bf16[16,48,96]{2,0,1:T(8,128)(2,1)} %copy.26), calls=%async_computation | async-start | bytes 393216 | tf_op jit(solution)/shard_map/all_to_all | solution.py:69
  79.3 6.6 %fusion = (bf16[2688,768]{1,0:T(8,128)(2,1)}, bf16[2688,768]{1,0:T(8,128)(2,1)}) fusion(bf16[21,128,768]{2,1,0:T(8,128)(2,1)} %get-tuple-element.9, pred[768]{0:T(1024)(128)(4,1)S(1)} %multiply_compare_fusion, pred[2688]{0:T(1024)(128)(4,1)S(1)} %iota_compare_fusion.5, bf16[21,128,768]{2,1,0:T(8,128)(2,1)} %get-tuple-element.10), kind=kLoop, calls=%fused_computation.2 | loop fusion | flops 6193152 | bytes 16518528 | tf_op jit(solution)/shard_map/convert.10
  85.8 1.2 dynamic_slice.11
  87.6 5.8 %all-to-all-done = bf16[16,48,96]{2,0,1:T(8,128)(2,1)S(1)} async-done(((bf16[16,48,96]{2,0,1:T(8,128)(2,1)}), bf16[16,48,96]{2,0,1:T(8,128)(2,1)S(1)}, u32[]{:S(2)}, u32[]{:S(2)}) %all-to-all-start) | async-done | bytes 147488 | tf_op jit(solution)/shard_map/all_to_all | solution.py:69
  93.5 0.9 copy.27
  94.3 0.9 reshape_squeeze.3
  95.5 5.3 %fusion.3 = f32[2688,96]{0,1:T(8,128)S(1)} fusion(bf16[2688,768]{1,0:T(8,128)(2,1)} %get-tuple-element.28, bf16[2688,768]{1,0:T(8,128)(2,1)} %get-tuple-element.27, bf16[768,48]{0,1:T(8,128)(2,1)S(1)} %get-tuple-element.29, bf16[768,48]{0,1:T(8,128)(2,1)S(1)} %get-tuple-element.30), kind=kOutput, calls=%fused_computation.8 | convolution fusion | flops 810418176 | bytes 9437184 | tf_op jit(solution)/shard_map/dot_general | solution.py:95
  101.6 0.6 pad_maximum_fusion.9
  103.1 0.6 pad_maximum_fusion.10
  104.0 4.4 %fusion.2 = f32[1536,96]{0,1:T(8,128)S(1)} fusion(bf16[2688,768]{1,0:T(8,128)(2,1)} %get-tuple-element.28, bf16[2688,768]{1,0:T(8,128)(2,1)} %get-tuple-element.27, bf16[2688,48]{0,1:T(8,128)(2,1)S(1)} %broadcast_select_fusion.1, bf16[2688,48]{0,1:T(8,128)(2,1)S(1)} %convert_element_type.61), kind=kOutput, calls=%fused_computation.7 | convolution fusion | flops 810270720 | bytes 9363456 | tf_op jit(solution)/shard_map/dot_general | solution.py:103
  108.7 0.5 broadcast.319
  109.2 0.7 reduce.2
  110.4 18.1 %all_to_all.35 = bf16[48,2,768]{2,1,0:T(2,128)(2,1)S(1)} all-to-all(bf16[48,2,768]{2,1,0:T(2,128)(2,1)S(1)} %reshape.287), channel_id=1, replica_groups=mesh['wave'=48,'lev'=16] {'wave'}, dimensions={0} | all-to-all | bytes 294912 | tf_op jit(solution)/shard_map/all_to_all | solution.py:112
  128.9 0.7 fusion.4
  129.6 1.1 copy.31
  130.7 55.4 %all_to_all.36 = bf16[16,6,8,1280]{3,2,1,0:T(8,128)(2,1)S(1)} all-to-all(bf16[16,6,8,1280]{3,2,1,0:T(8,128)(2,1)S(1)} %bitcast.56), channel_id=1, replica_groups=mesh['wave'=48,'lev'=16] {'lev'}, dimensions={0} | all-to-all | bytes 3932160 | tf_op jit(solution)/shard_map/all_to_all | solution.py:121
  186.4 0.8 rev.11
  187.6 1.1 reshape.283
  (42 shorter events, 5.0 us)
Async XLA Ops:
  6.5 56.6 %all-gather.2.cloned.1.call-start = ((), (), s32[]{:S(2)}) async-start(), calls=%async_computation.3 | async-start | bytes 2088960 | tf_op jit(solution)/shard_map/all_gather | solution.py:64
  8.6 11.9 %copy-start.2 = (s32[768]{0:T(1024)S(1)}, s32[768]{0:T(1024)}, u32[]{:S(2)}) copy-start(s32[768]{0:T(1024)} %param.9) | copy-start | bytes 9220
  27.6 35.5 %copy-start = (bf16[8,1,48,1280]{3,2,1,0:T(8,128)(2,1)S(1)}, bf16[8,1,48,1280]{3,2,1,0:T(8,128)(2,1)}, u32[]{:S(2)}) copy-start(bf16[8,1,48,1280]{3,2,1,0:T(8,128)(2,1)} %get-tuple-element.5) | copy-start | bytes 2949124
  66.1 27.4 %all-to-all-start = ((bf16[16,48,96]{2,0,1:T(8,128)(2,1)}), bf16[16,48,96]{2,0,1:T(8,128)(2,1)S(1)}, u32[]{:S(2)}, u32[]{:S(2)}) async-start(bf16[16,48,96]{2,0,1:T(8,128)(2,1)} %copy.26), calls=%async_computation | async-start | bytes 393216 | tf_op jit(solution)/shard_map/all_to_all | solution.py:69
  108.4 20.4 %copy-start.1 = (bf16[8,1,48,1280]{3,2,1,0:T(8,128)(2,1)S(1)}, bf16[8,1,48,1280]{3,2,1,0:T(8,128)(2,1)}, u32[]{:S(2)}) copy-start(bf16[8,1,48,1280]{3,2,1,0:T(8,128)(2,1)} %get-tuple-element.5) | copy-start | bytes 2949124
Sparse Core Ops, SparseCore 0:
  10.7 52.3 all-gather.1

commit v4 on v3

--- a/solution.py
+++ b/solution.py
@@ -8,6 +8,7 @@
 TRUNC = 1279
 LON_BLOCK = 768
 NLONPAD = 5376
+LEV = ("chip", "core")
 
 
 def angle_parts(count, waves, starts):
@@ -45,7 +46,7 @@
 
 def per_device(spectral, legendre, weights, nlon, assignment):
     wave_index = lax.axis_index("wave")
-    lev_index = lax.axis_index("lev")
+    lev_index = lax.axis_index("chip") * lax.axis_size("core") + lax.axis_index("core")
     slots = legendre.shape[0]
     lat_band = legendre.shape[1]
     kmax_width = legendre.shape[2]
@@ -61,7 +62,7 @@
     packed_leg = jnp.stack([leg_a, leg_b], axis=1)
     spec_pairs = spectral.reshape(spectral.shape[0], pairs_n, 2, kmax_width)
     packed_spec = jnp.where(front[None], spec_pairs[:, :, 0], spec_pairs[:, :, 1, ::-1])
-    spec_all = lax.all_gather(packed_spec, "lev", axis=0, tiled=True)
+    spec_all = lax.all_gather(packed_spec, LEV, axis=0, tiled=True)
     columns = spec_all.shape[0]
     four_local = jnp.einsum(
         "pxlk,cpk->pxlc", packed_leg, spec_all, preferred_element_type=jnp.float32
@@ -114,11 +115,17 @@
     band_term = jnp.einsum(
         "pxlc,pxlk->cpk", returned, packed_leg, preferred_element_type=jnp.float32
     )
-    lev_count = lax.axis_size("lev")
+    chips = lax.axis_size("chip")
+    cores = lax.axis_size("core")
+    core_index = lax.axis_index("core")
     shares = band_term.astype(jnp.bfloat16).reshape(
-        lev_count, columns // lev_count, pairs_n, kmax_width
+        chips, cores, columns // (chips * cores), pairs_n, kmax_width
     )
-    gathered = lax.all_to_all(shares, "lev", split_axis=0, concat_axis=0, tiled=True)
+    keep = lax.dynamic_index_in_dim(shares, core_index, axis=1, keepdims=False)
+    give = lax.dynamic_index_in_dim(shares, cores - 1 - core_index, axis=1, keepdims=False)
+    got = lax.ppermute(give, "core", [(0, 1), (1, 0)])
+    pair_sum = (keep.astype(jnp.float32) + got.astype(jnp.float32)).astype(jnp.bfloat16)
+    gathered = lax.all_to_all(pair_sum, "chip", split_axis=0, concat_axis=0, tiled=True)
     summed = jnp.sum(gathered.astype(jnp.float32), axis=0)
     zero_f = jnp.zeros((), jnp.float32)
     out_a = jnp.where(front[None], summed, zero_f)
@@ -128,10 +135,12 @@
 
 
 def solution(mesh):
+    grid = mesh.devices.reshape(mesh.shape["wave"], mesh.shape["lev"] // 2, 2)
+    split_mesh = jax.sharding.Mesh(grid, ("wave", "chip", "core"))
     return jax.shard_map(
         per_device,
-        mesh=mesh,
-        in_specs=(P("lev", "wave", None), P("wave", "lev", None), P(), P(), P()),
-        out_specs=P("lev", "wave", None),
+        mesh=split_mesh,
+        in_specs=(P(LEV, "wave", None), P("wave", LEV, None), P(), P(), P()),
+        out_specs=P(LEV, "wave", None),
         check_vma=False,
     )

time: 196 us -> 181 us (0.923)
  blocking collectives: 73.5 us -> 30.5 us
  waiting for transfers between devices: 36.6 us -> 50.7 us
  starting transfers between devices: 13.2 us -> 24.2 us
    all_to_all x2 -> x1, blocking collectives: 73.5 us -> 30.5 us  [per_device(): lax.all_to_all(pair_sum, 'chip', split_axis=0, concat_axis=0, tiled=True)]
    all_to_all x0 -> x1, waiting for transfers between devices: none -> 12.4 us  [per_device(): lax.all_to_all(analysed, 'wave', split_axis=0, concat_axis=1, tiled=True)]
    all_to_all x0 -> x1, starting transfers between devices: none -> 6.05 us  [per_device(): lax.all_to_all(analysed, 'wave', split_axis=0, concat_axis=1, tiled=True)]
    ppermute x0 -> x1, starting transfers between devices: none -> 4.95 us  [per_device(): got = lax.ppermute(give, 'core', [(0, 1), (1, 0)])]
    ppermute x0 -> x1, waiting for transfers between devices: none -> 2.38 us  [per_device(): got = lax.ppermute(give, 'core', [(0, 1), (1, 0)])]
  transfers between devices with their start and end apart: 2 -> 4, of which waited for: 2 -> 4; matrix products, arithmetic and copies ran while one was open for 13% -> 14% of each run, Pallas kernels for 0% -> 0%
where the time goes in v4:
time: 181 us; the launch traced here: 180 us
  waiting for transfers between devices  50.7 us (28%)
  blocking collectives  30.5 us (17%)
  other arithmetic  25.7 us (14%)
  starting transfers between devices  24.2 us (13%)
  between operations  19.2 us (11%)
  local copies, waits for them, and re-layouts  17.3 us (10%)
  matrix products  12.6 us (7%)
    all_to_all x1, blocking collectives, per_device(): lax.all_to_all(pair_sum, 'chip', split_axis=0, concat_axis=0, tiled=True)  30.5 us
    all_gather x1, waiting for transfers between devices, per_device(): spec_all = lax.all_gather(packed_spec, LEV, axis=0, tiled=True)  30.2 us
    all_to_all x1, starting transfers between devices, per_device(): lax.all_to_all(four_local, 'wave', split_axis=1, concat_axis=0, tiled=True)  13.2 us
    all_to_all x1, waiting for transfers between devices, per_device(): lax.all_to_all(analysed, 'wave', split_axis=0, concat_axis=1, tiled=True)  12.4 us
    another operation x3, other arithmetic  7.53 us
    cos x2, other arithmetic, angle_parts(): return (jnp.cos(angle), jnp.sin(angle))  6.37 us
    all_to_all x1, starting transfers between devices, per_device(): lax.all_to_all(analysed, 'wave', split_axis=0, concat_axis=1, tiled=True)  6.05 us
    all_to_all x1, waiting for transfers between devices, per_device(): lax.all_to_all(four_local, 'wave', split_axis=1, concat_axis=0, tiled=True)  5.7 us
  transfers between devices with their start and end apart: 4, of which 4 were waited for; matrix products, arithmetic and copies ran while one was open for 14% of the time, Pallas kernels for 0%

profile of v4, /device:TPU:1, one launch (start us, length us, event | category | flops | bytes accessed | tf_op | source)
XLA Modules:
  0.0 180.1 jit_solution(10942303209671869588)
XLA Ops:
  6.5 0.8 dynamic_slice.16
  7.6 1.0 reshape.279
  9.0 0.9 rev.10
  10.6 1.3 dynamic_slice.17
  16.7 2.6 %slice_select_fusion = (bf16[8,1,48,1280]{3,2,1,0:T(8,128)(2,1)}, bf16[8,1,48,1280]{3,2,1,0:T(8,128)(2,1)S(1)}) fusion(bf16[8,2,48,1280]{3,2,1,0:T(8,128)(2,1)} %bitcast.63, pred[8,1280]{1,0:T(8,128)(4,1)S(1)} %iota_compare_fusion.2), kind=kLoop, calls=%fused_computation.18 | loop fusion | flops 491520 | bytes 3942400 | tf_op jit(solution)/shard_map/jit(_where)/select_n | solution.py:60
  19.3 1.4 rev.9
  20.9 0.7 multiply_compare_fusion
  21.6 1.1 fusion.47
  22.7 5.3 %fusion.30 = (f32[128,768]{1,0:T(8,128)S(1)}, f32[128,768]{1,0:T(8,128)S(1)}) fusion(f32[]{:T(128)S(6)} %convert_element_type.70, pred[]{:T(512)S(6)} %lt.126, s32[]{:T(128)S(6)} %select_n.114, s32[768]{0:T(1024)S(1)} %copy-done.2, s32[128]{0:T(128)S(1)} %and_select_fusion.2), kind=kLoop, calls=%fused_computation.49 | loop fusion | flops 1081344 | bytes 790025 | tf_op jit(solution)/shard_map/cos | solution.py:17
  28.1 4.8 %multiply_subtract_fusion = (bf16[21,128,768]{2,1,0:T(8,128)(2,1)}, bf16[21,128,768]{2,1,0:T(8,128)(2,1)}) fusion(f32[128,768]{1,0:T(8,128)S(1)} %get-tuple-element.26, f32[21,768]{1,0:T(8,128)S(1)} %get-tuple-element.24, f32[128,768]{1,0:T(8,128)S(1)} %get-tuple-element.25, f32[21,768]{1,0:T(8,128)S(1)} %get-tuple-element.23), kind=kLoop, calls=%fused_computation.6 | loop fusion | flops 18579456 | bytes 9172992 | tf_op jit(solution)/shard_map/sub | solution.py:22
  32.9 30.2 %all-gather.2.cloned.1.call-done = bf16[96,8,1280]{2,1,0:T(8,128)(2,1)} async-done(((bf16[6,8,1280]{2,1,0:T(8,128)(2,1)}), bf16[96,8,1280]{2,1,0:T(8,128)(2,1)}) %all-gather.2.cloned.1.call-update) | async-done | bytes 1966096 | tf_op jit(solution)/shard_map/all_gather | solution.py:65
  63.1 2.2 %fusion.8 = bf16[8,2,48,96]{3,2,1,0:T(8,128)(2,1)S(1)} fusion(bf16[96,8,1280,1]{2,1,0,3:T(8,128)(2,1)} %bitcast.69, bf16[8,1,48,1280]{3,2,1,0:T(8,128)(2,1)S(1)} %broadcast_select_fusion, bf16[8,1,48,1280]{3,2,1,0:T(8,128)(2,1)S(1)} %copy-done), kind=kOutput, calls=%fused_computation.17 | convolution fusion | flops 189800448 | bytes 4079616 | tf_op jit(solution)/shard_map/pxlk,cpk->pxlc/dot_general | solution.py:67
  65.3 0.7 copy.26
  66.1 13.2 %all-to-all-start = ((bf16[16,48,96]{2,0,1:T(8,128)(2,1)}), bf16[16,48,96]{2,0,1:T(8,128)(2,1)S(1)}, u32[]{:S(2)}, u32[]{:S(2)}) async-start(bf16[16,48,96]{2,0,1:T(8,128)(2,1)} %copy.26), calls=%async_computation | async-start | bytes 393216 | tf_op jit(solution)/shard_map/all_to_all | solution.py:70
  79.3 6.6 %fusion = (bf16[2688,768]{1,0:T(8,128)(2,1)}, bf16[2688,768]{1,0:T(8,128)(2,1)}) fusion(bf16[21,128,768]{2,1,0:T(8,128)(2,1)} %get-tuple-element.9, pred[768]{0:T(1024)(128)(4,1)S(1)} %multiply_compare_fusion, pred[2688]{0:T(1024)(128)(4,1)S(1)} %iota_compare_fusion.5, bf16[21,128,768]{2,1,0:T(8,128)(2,1)} %get-tuple-element.10), kind=kLoop, calls=%fused_computation.2 | loop fusion | flops 6193152 | bytes 16518528 | tf_op jit(solution)/shard_map/convert.11
  85.8 1.3 dynamic_slice.18
  87.8 5.7 %all-to-all-done = bf16[16,48,96]{2,0,1:T(8,128)(2,1)S(1)} async-done(((bf16[16,48,96]{2,0,1:T(8,128)(2,1)}), bf16[16,48,96]{2,0,1:T(8,128)(2,1)S(1)}, u32[]{:S(2)}, u32[]{:S(2)}) %all-to-all-start) | async-done | bytes 147488 | tf_op jit(solution)/shard_map/all_to_all | solution.py:70
  93.5 0.9 copy.27
  94.3 0.9 reshape_squeeze.3
  95.5 5.2 %fusion.3 = f32[2688,96]{0,1:T(8,128)S(1)} fusion(bf16[2688,768]{1,0:T(8,128)(2,1)} %get-tuple-element.28, bf16[2688,768]{1,0:T(8,128)(2,1)} %get-tuple-element.27, bf16[768,48]{0,1:T(8,128)(2,1)S(1)} %get-tuple-element.29, bf16[768,48]{0,1:T(8,128)(2,1)S(1)} %get-tuple-element.30), kind=kOutput, calls=%fused_computation.8 | convolution fusion | flops 810418176 | bytes 9437184 | tf_op jit(solution)/shard_map/dot_general | solution.py:96
  104.0 4.4 %fusion.2 = f32[1536,96]{0,1:T(8,128)S(1)} fusion(bf16[2688,768]{1,0:T(8,128)(2,1)} %get-tuple-element.28, bf16[2688,768]{1,0:T(8,128)(2,1)} %get-tuple-element.27, bf16[2688,48]{0,1:T(8,128)(2,1)S(1)} %broadcast_select_fusion.1, bf16[2688,48]{0,1:T(8,128)(2,1)S(1)} %convert_element_type.73), kind=kOutput, calls=%fused_computation.7 | convolution fusion | flops 810270720 | bytes 9363456 | tf_op jit(solution)/shard_map/dot_general | solution.py:104
  110.1 1.0 reshape.290
  111.0 6.0 %all-to-all-start.1 = ((bf16[48,2,768]{2,1,0:T(2,128)(2,1)}), bf16[48,2,768]{2,1,0:T(2,128)(2,1)S(1)}, u32[]{:S(2)}, u32[]{:S(2)}) async-start(bf16[48,2,768]{2,1,0:T(2,128)(2,1)} %reshape.290), calls=%async_computation.1 | async-start | bytes 294912 | tf_op jit(solution)/shard_map/all_to_all | solution.py:113
  117.1 12.4 %all-to-all-done.1 = bf16[48,2,768]{2,1,0:T(2,128)(2,1)S(1)} async-done(((bf16[48,2,768]{2,1,0:T(2,128)(2,1)}), bf16[48,2,768]{2,1,0:T(2,128)(2,1)S(1)}, u32[]{:S(2)}, u32[]{:S(2)}) %all-to-all-start.1) | async-done | bytes 147488 | tf_op jit(solution)/shard_map/all_to_all | solution.py:113
  129.8 0.7 fusion.4
  130.6 1.1 copy.31
  131.7 1.0 dynamic-slice_bitcast_fusion
  132.7 5.0 %collective-permute-start = (bf16[8,6,8,1280]{3,2,1,0:T(8,128)(2,1)}, bf16[8,6,8,1280]{3,2,1,0:T(8,128)(2,1)S(1)}, u32[]{:S(2)}, u32[]{:S(2)}) collective-permute-start(bf16[8,6,8,1280]{3,2,1,0:T(8,128)(2,1)} %dynamic-slice_bitcast_fusion), channel_id=1, source_target_pairs={{0,1},{1,0},{2,3},{3,2},{4,5},{5,4},{6,7},{7,6},{8,9},{9,8},{10,11... | collective-permute-start | bytes 2949128 | tf_op jit(solution)/shard_map/ppermute | solution.py:126
  137.6 2.4 %collective-permute-done = bf16[8,6,8,1280]{3,2,1,0:T(8,128)(2,1)S(1)} collective-permute-done((bf16[8,6,8,1280]{3,2,1,0:T(8,128)(2,1)}, bf16[8,6,8,1280]{3,2,1,0:T(8,128)(2,1)S(1)}, u32[]{:S(2)}, u32[]{:S(2)}) %collective-permute-start) | collective-permute-done | bytes 983072 | tf_op jit(solution)/shard_map/ppermute | solution.py:126
  140.3 30.5 %all_to_all.35 = bf16[8,6,8,1280]{3,2,1,0:T(8,128)(2,1)S(1)} all-to-all(bf16[8,6,8,1280]{3,2,1,0:T(8,128)(2,1)S(1)} %fusion.5), channel_id=1, replica_groups=mesh['wave'=48,'chip'=8,'core'=2] {'chip'}, dimensions={0} | all-to-all | bytes 1966080 | tf_op jit(solution)/shard_map/all_to_all | solution.py:128
  171.0 0.8 rev.11
  172.2 1.1 reshape.285
  (47 shorter events, 7.9 us)
Async XLA Ops:
  6.5 56.6 %all-gather.2.cloned.1.call-start = ((), (), s32[]{:S(2)}) async-start(), calls=%async_computation.3 | async-start | bytes 2088960 | tf_op jit(solution)/shard_map/all_gather | solution.py:65
  8.6 12.3 %copy-start.2 = (s32[768]{0:T(1024)S(1)}, s32[768]{0:T(1024)}, u32[]{:S(2)}) copy-start(s32[768]{0:T(1024)} %param.9) | copy-start | bytes 9220
  28.1 35.0 %copy-start = (bf16[8,1,48,1280]{3,2,1,0:T(8,128)(2,1)S(1)}, bf16[8,1,48,1280]{3,2,1,0:T(8,128)(2,1)}, u32[]{:S(2)}) copy-start(bf16[8,1,48,1280]{3,2,1,0:T(8,128)(2,1)} %get-tuple-element.5) | copy-start | bytes 2949124
  66.1 27.4 %all-to-all-start = ((bf16[16,48,96]{2,0,1:T(8,128)(2,1)}), bf16[16,48,96]{2,0,1:T(8,128)(2,1)S(1)}, u32[]{:S(2)}, u32[]{:S(2)}) async-start(bf16[16,48,96]{2,0,1:T(8,128)(2,1)} %copy.26), calls=%async_computation | async-start | bytes 393216 | tf_op jit(solution)/shard_map/all_to_all | solution.py:70
  108.4 21.4 %copy-start.1 = (bf16[8,1,48,1280]{3,2,1,0:T(8,128)(2,1)S(1)}, bf16[8,1,48,1280]{3,2,1,0:T(8,128)(2,1)}, u32[]{:S(2)}) copy-start(bf16[8,1,48,1280]{3,2,1,0:T(8,128)(2,1)} %get-tuple-element.5) | copy-start | bytes 2949124
  111.0 18.4 %all-to-all-start.1 = ((bf16[48,2,768]{2,1,0:T(2,128)(2,1)}), bf16[48,2,768]{2,1,0:T(2,128)(2,1)S(1)}, u32[]{:S(2)}, u32[]{:S(2)}) async-start(bf16[48,2,768]{2,1,0:T(2,128)(2,1)} %reshape.290), calls=%async_computation.1 | async-start | bytes 294912 | tf_op jit(solution)/shard_map/all_to_all | solution.py:113
  132.7 7.3 %collective-permute-start = (bf16[8,6,8,1280]{3,2,1,0:T(8,128)(2,1)}, bf16[8,6,8,1280]{3,2,1,0:T(8,128)(2,1)S(1)}, u32[]{:S(2)}, u32[]{:S(2)}) collective-permute-start(bf16[8,6,8,1280]{3,2,1,0:T(8,128)(2,1)} %dynamic-slice_bitcast_fusion), channel_id=1, source_target_pairs={{0,1},{1,0},{2,3},{3,2},{4,5},{5,4},{6,7},{7,6},{8,9},{9,8},{10,11... | collective-permute-start | bytes 2949128 | tf_op jit(solution)/shard_map/ppermute | solution.py:126
Sparse Core Ops, SparseCore 0:
  10.7 52.3 all-gather.1

commit v5 on v4

--- a/solution.py
+++ b/solution.py
@@ -42,6 +42,27 @@
     temper = fields[:, :, 2]
     stacked = jnp.stack([vort * temper, diverg * temper, vort * diverg], axis=-1)
     return stacked.reshape(grid.shape[0], grid.shape[1]).astype(jnp.bfloat16)
+
+
+def ring_reduce(shares, axis):
+    size = lax.axis_size(axis)
+    me = lax.axis_index(axis)
+    half = shares.shape[-1] // 2
+    lanes = (shares[..., :half], shares[..., half:])
+    steps = ((1, [(i, (i + 1) % size) for i in range(size)]),
+             (-1, [(i, (i - 1) % size) for i in range(size)]))
+    ends = []
+    for lane, (sign, perm) in zip(lanes, steps):
+        acc = lax.dynamic_index_in_dim(lane, (me - sign) % size, axis=0, keepdims=False)
+        acc = acc.astype(jnp.float32)
+        for step in range(size - 1):
+            moved = lax.ppermute(acc.astype(jnp.bfloat16), axis, perm)
+            mine = lax.dynamic_index_in_dim(
+                lane, (me - sign * (step + 2)) % size, axis=0, keepdims=False
+            )
+            acc = moved.astype(jnp.float32) + mine.astype(jnp.float32)
+        ends.append(acc)
+    return jnp.concatenate(ends, axis=-1)
 
 
 def per_device(spectral, legendre, weights, nlon, assignment):
@@ -125,8 +146,7 @@
     give = lax.dynamic_index_in_dim(shares, cores - 1 - core_index, axis=1, keepdims=False)
     got = lax.ppermute(give, "core", [(0, 1), (1, 0)])
     pair_sum = (keep.astype(jnp.float32) + got.astype(jnp.float32)).astype(jnp.bfloat16)
-    gathered = lax.all_to_all(pair_sum, "chip", split_axis=0, concat_axis=0, tiled=True)
-    summed = jnp.sum(gathered.astype(jnp.float32), axis=0)
+    summed = ring_reduce(pair_sum, "chip")
     zero_f = jnp.zeros((), jnp.float32)
     out_a = jnp.where(front[None], summed, zero_f)
     out_b = jnp.where(front[None], zero_f, summed)[:, :, ::-1]

time: 181 us -> 204 us (1.13)
  the two profiles are of different devices: /device:TPU:1 before, /device:TPU:24 now
where the time goes in v5:
time: 204 us; the launch traced here: 203 us
  starting transfers between devices  67.8 us (33%)
  waiting for transfers between devices  58.4 us (29%)
  other arithmetic  25.9 us (13%)
  between operations  19.7 us (10%)
  local copies, waits for them, and re-layouts  18.4 us (9%)
  matrix products  12.6 us (6%)
    ppermute x14, starting transfers between devices, ring_reduce(): moved = lax.ppermute(acc.astype(jnp.bfloat16), axis, perm)  47.4 us
    all_gather x1, waiting for transfers between devices, per_device(): spec_all = lax.all_gather(packed_spec, LEV, axis=0, tiled=True)  28.6 us
    all_to_all x1, waiting for transfers between devices, per_device(): lax.all_to_all(analysed, 'wave', split_axis=0, concat_axis=1, tiled=True)  14.1 us
    all_to_all x1, starting transfers between devices, per_device(): lax.all_to_all(four_local, 'wave', split_axis=1, concat_axis=0, tiled=True)  13.3 us
    another operation x3, other arithmetic  7.55 us
    all_to_all x1, waiting for transfers between devices, per_device(): lax.all_to_all(four_local, 'wave', split_axis=1, concat_axis=0, tiled=True)  7.45 us
    cos x2, other arithmetic, angle_parts(): return (jnp.cos(angle), jnp.sin(angle))  6.37 us
    ppermute x14, waiting for transfers between devices, ring_reduce(): moved = lax.ppermute(acc.astype(jnp.bfloat16), axis, perm)  5.92 us
  transfers between devices with their start and end apart: 18, of which 7 were waited for; matrix products, arithmetic and copies ran while one was open for 13% of the time, Pallas kernels for 0%

profile of v5, /device:TPU:24, one launch (start us, length us, event | category | flops | bytes accessed | tf_op | source)
XLA Modules:
  0.0 202.8 jit_solution(9237504570912332873)
XLA Ops:
  9.0 1.8 rev.10
  11.5 1.4 dynamic_slice.66
  17.7 2.6 %slice_select_fusion = (bf16[8,1,48,1280]{3,2,1,0:T(8,128)(2,1)}, bf16[8,1,48,1280]{3,2,1,0:T(8,128)(2,1)S(1)}) fusion(bf16[8,2,48,1280]{3,2,1,0:T(8,128)(2,1)} %bitcast.109, pred[8,1280]{1,0:T(8,128)(4,1)S(1)} %iota_compare_fusion.2), kind=kLoop, calls=%fused_computation.17 | loop fusion | flops 491520 | bytes 3942400 | tf_op jit(solution)/shard_map/jit(_where)/select_n | solution.py:81
  20.3 1.4 rev.9
  23.8 5.3 %fusion.30 = (f32[128,768]{1,0:T(8,128)S(1)}, f32[128,768]{1,0:T(8,128)S(1)}) fusion(f32[]{:T(128)S(6)} %convert_element_type.233, pred[]{:T(512)S(6)} %lt.241, s32[]{:T(128)S(6)} %select_n.229, s32[768]{0:T(1024)S(1)} %copy-done.2, s32[128]{0:T(128)S(1)} %and_select_fusion.2), kind=kLoop, calls=%fused_computation.49 | loop fusion | flops 1081344 | bytes 790025 | tf_op jit(solution)/shard_map/cos | solution.py:17
  29.2 4.7 %multiply_subtract_fusion = (bf16[21,128,768]{2,1,0:T(8,128)(2,1)}, bf16[21,128,768]{2,1,0:T(8,128)(2,1)}) fusion(f32[128,768]{1,0:T(8,128)S(1)} %get-tuple-element.28, f32[21,768]{1,0:T(8,128)S(1)} %get-tuple-element.26, f32[128,768]{1,0:T(8,128)S(1)} %get-tuple-element.27, f32[21,768]{1,0:T(8,128)S(1)} %get-tuple-element.25), kind=kLoop, calls=%fused_computation.6 | loop fusion | flops 18579456 | bytes 9172992 | tf_op jit(solution)/shard_map/sub | solution.py:22
  33.9 28.6 %all-gather.2.cloned.1.call-done = bf16[96,8,1280]{2,1,0:T(8,128)(2,1)} async-done(((bf16[6,8,1280]{2,1,0:T(8,128)(2,1)}), bf16[96,8,1280]{2,1,0:T(8,128)(2,1)}) %all-gather.2.cloned.1.call-update) | async-done | bytes 1966096 | tf_op jit(solution)/shard_map/all_gather | solution.py:86
  62.6 2.2 %fusion.8 = bf16[8,2,48,96]{3,2,1,0:T(8,128)(2,1)S(1)} fusion(bf16[96,8,1280,1]{2,1,0,3:T(8,128)(2,1)} %bitcast.117, bf16[8,1,48,1280]{3,2,1,0:T(8,128)(2,1)S(1)} %broadcast_select_fusion, bf16[8,1,48,1280]{3,2,1,0:T(8,128)(2,1)S(1)} %copy-done), kind=kOutput, calls=%fused_computation.16 | convolution fusion | flops 189800448 | bytes 4079616 | tf_op jit(solution)/shard_map/pxlk,cpk->pxlc/dot_general | solution.py:88
  65.5 13.3 %all-to-all-start = ((bf16[16,48,96]{2,0,1:T(8,128)(2,1)}), bf16[16,48,96]{2,0,1:T(8,128)(2,1)S(1)}, u32[]{:S(2)}, u32[]{:S(2)}) async-start(bf16[16,48,96]{2,0,1:T(8,128)(2,1)} %copy.47), calls=%async_computation | async-start | bytes 393216 | tf_op jit(solution)/shard_map/all_to_all | solution.py:91
  78.8 6.6 %fusion = (bf16[2688,768]{1,0:T(8,128)(2,1)}, bf16[2688,768]{1,0:T(8,128)(2,1)}) fusion(bf16[21,128,768]{2,1,0:T(8,128)(2,1)} %get-tuple-element.11, pred[768]{0:T(1024)(128)(4,1)S(1)} %multiply_compare_fusion, pred[2688]{0:T(1024)(128)(4,1)S(1)} %iota_compare_fusion.5, bf16[21,128,768]{2,1,0:T(8,128)(2,1)} %get-tuple-element.12), kind=kLoop, calls=%fused_computation.2 | loop fusion | flops 6193152 | bytes 16518528 | tf_op jit(solution)/shard_map/convert.25
  87.3 7.5 %all-to-all-done = bf16[16,48,96]{2,0,1:T(8,128)(2,1)S(1)} async-done(((bf16[16,48,96]{2,0,1:T(8,128)(2,1)}), bf16[16,48,96]{2,0,1:T(8,128)(2,1)S(1)}, u32[]{:S(2)}, u32[]{:S(2)}) %all-to-all-start) | async-done | bytes 147488 | tf_op jit(solution)/shard_map/all_to_all | solution.py:91
  96.8 5.3 %fusion.3 = f32[2688,96]{0,1:T(8,128)S(1)} fusion(bf16[2688,768]{1,0:T(8,128)(2,1)} %get-tuple-element.30, bf16[2688,768]{1,0:T(8,128)(2,1)} %get-tuple-element.29, bf16[768,48]{0,1:T(8,128)(2,1)S(1)} %get-tuple-element.31, bf16[768,48]{0,1:T(8,128)(2,1)S(1)} %get-tuple-element.32), kind=kOutput, calls=%fused_computation.8 | convolution fusion | flops 810418176 | bytes 9437184 | tf_op jit(solution)/shard_map/dot_general | solution.py:117
  105.3 4.4 %fusion.2 = f32[1536,96]{0,1:T(8,128)S(1)} fusion(bf16[2688,768]{1,0:T(8,128)(2,1)} %get-tuple-element.30, bf16[2688,768]{1,0:T(8,128)(2,1)} %get-tuple-element.29, bf16[2688,48]{0,1:T(8,128)(2,1)S(1)} %broadcast_select_fusion.1, bf16[2688,48]{0,1:T(8,128)(2,1)S(1)} %convert_element_type.236), kind=kOutput, calls=%fused_computation.7 | convolution fusion | flops 810270720 | bytes 9363456 | tf_op jit(solution)/shard_map/dot_general | solution.py:125
  112.3 5.0 %all-to-all-start.1 = ((bf16[48,2,768]{2,1,0:T(2,128)(2,1)}), bf16[48,2,768]{2,1,0:T(2,128)(2,1)S(1)}, u32[]{:S(2)}, u32[]{:S(2)}) async-start(bf16[48,2,768]{2,1,0:T(2,128)(2,1)} %reshape.354), calls=%async_computation.1 | async-start | bytes 294912 | tf_op jit(solution)/shard_map/all_to_all | solution.py:134
  117.3 14.1 %all-to-all-done.1 = bf16[48,2,768]{2,1,0:T(2,128)(2,1)S(1)} async-done(((bf16[48,2,768]{2,1,0:T(2,128)(2,1)}), bf16[48,2,768]{2,1,0:T(2,128)(2,1)S(1)}, u32[]{:S(2)}, u32[]{:S(2)}) %all-to-all-start.1) | async-done | bytes 147488 | tf_op jit(solution)/shard_map/all_to_all | solution.py:134
  134.7 2.1 %collective-permute-start = (bf16[8,6,8,1280]{3,2,1,0:T(8,128)(2,1)}, bf16[8,6,8,1280]{3,2,1,0:T(8,128)(2,1)S(1)}, u32[]{:S(2)}, u32[]{:S(2)}) collective-permute-start(bf16[8,6,8,1280]{3,2,1,0:T(8,128)(2,1)} %dynamic-slice_bitcast_fusion), channel_id=1, source_target_pairs={{0,1},{1,0},{2,3},{3,2},{4,5},{5,4},{6,7},{7,6},{8,9},{9,8},{10,11... | collective-permute-start | bytes 2949128 | tf_op jit(solution)/shard_map/ppermute | solution.py:147
  137.1 2.2 %collective-permute-done = bf16[8,6,8,1280]{3,2,1,0:T(8,128)(2,1)S(1)} collective-permute-done((bf16[8,6,8,1280]{3,2,1,0:T(8,128)(2,1)}, bf16[8,6,8,1280]{3,2,1,0:T(8,128)(2,1)S(1)}, u32[]{:S(2)}, u32[]{:S(2)}) %collective-permute-start) | collective-permute-done | bytes 983072 | tf_op jit(solution)/shard_map/ppermute | solution.py:147
  139.7 2.3 %collective-permute-start.1 = (bf16[6,8,640]{2,1,0:T(8,128)(2,1)S(1)}, bf16[6,8,640]{2,1,0:T(8,128)(2,1)S(1)}, u32[]{:S(2)}, u32[]{:S(2)}) collective-permute-start(bf16[6,8,640]{2,1,0:T(8,128)(2,1)S(1)} %dynamic-slice_bitcast_fusion.2), channel_id=1, source_target_pairs={{0,2},{2,4},{4,6},{6,8},{8,10},{10,12},{12,14},{14,0},{1,3},{3,5},... | collective-permute-start | bytes 184328 | tf_op jit(solution)/shard_map/ppermute | solution.py:59
  142.1 3.5 %collective-permute-start.8 = (bf16[6,8,640]{2,1,0:T(8,128)(2,1)S(1)}, bf16[6,8,640]{2,1,0:T(8,128)(2,1)S(1)}, u32[]{:S(2)}, u32[]{:S(2)}) collective-permute-start(bf16[6,8,640]{2,1,0:T(8,128)(2,1)S(1)} %dynamic-slice_bitcast_fusion.1), channel_id=1, source_target_pairs={{0,14},{2,0},{4,2},{6,4},{8,6},{10,8},{12,10},{14,12},{1,15},{3,1}... | collective-permute-start | bytes 184328 | tf_op jit(solution)/shard_map/ppermute | solution.py:59
  145.9 3.5 %collective-permute-start.2 = (bf16[6,8,640]{2,1,0:T(8,128)(2,1)S(1)}, bf16[6,8,640]{2,1,0:T(8,128)(2,1)S(1)}, u32[]{:S(2)}, u32[]{:S(2)}) collective-permute-start(bf16[6,8,640]{2,1,0:T(8,128)(2,1)S(1)} %fusion.47), channel_id=1, source_target_pairs={{0,2},{2,4},{4,6},{6,8},{8,10},{10,12},{12,14},{14,0},{1,3},{3,5},... | collective-permute-start | bytes 184328 | tf_op jit(solution)/shard_map/ppermute | solution.py:59
  149.5 2.3 %collective-permute-start.9 = (bf16[6,8,640]{2,1,0:T(8,128)(2,1)S(1)}, bf16[6,8,640]{2,1,0:T(8,128)(2,1)S(1)}, u32[]{:S(2)}, u32[]{:S(2)}) collective-permute-start(bf16[6,8,640]{2,1,0:T(8,128)(2,1)S(1)} %fusion.41), channel_id=1, source_target_pairs={{0,14},{2,0},{4,2},{6,4},{8,6},{10,8},{12,10},{14,12},{1,15},{3,1}... | collective-permute-start | bytes 184328 | tf_op jit(solution)/shard_map/ppermute | solution.py:59
  152.0 4.8 %collective-permute-start.3 = (bf16[6,8,640]{2,1,0:T(8,128)(2,1)S(1)}, bf16[6,8,640]{2,1,0:T(8,128)(2,1)S(1)}, u32[]{:S(2)}, u32[]{:S(2)}) collective-permute-start(bf16[6,8,640]{2,1,0:T(8,128)(2,1)S(1)} %fusion.46), channel_id=1, source_target_pairs={{0,2},{2,4},{4,6},{6,8},{8,10},{10,12},{12,14},{14,0},{1,3},{3,5},... | collective-permute-start | bytes 184328 | tf_op jit(solution)/shard_map/ppermute | solution.py:59
  156.8 1.9 collective-permute-start.10
  158.8 5.3 %collective-permute-start.4 = (bf16[6,8,640]{2,1,0:T(8,128)(2,1)S(1)}, bf16[6,8,640]{2,1,0:T(8,128)(2,1)S(1)}, u32[]{:S(2)}, u32[]{:S(2)}) collective-permute-start(bf16[6,8,640]{2,1,0:T(8,128)(2,1)S(1)} %fusion.45), channel_id=1, source_target_pairs={{0,2},{2,4},{4,6},{6,8},{8,10},{10,12},{12,14},{14,0},{1,3},{3,5},... | collective-permute-start | bytes 184328 | tf_op jit(solution)/shard_map/ppermute | solution.py:59
  164.2 1.9 collective-permute-start.11
  166.1 5.3 %collective-permute-start.5 = (bf16[6,8,640]{2,1,0:T(8,128)(2,1)S(1)}, bf16[6,8,640]{2,1,0:T(8,128)(2,1)S(1)}, u32[]{:S(2)}, u32[]{:S(2)}) collective-permute-start(bf16[6,8,640]{2,1,0:T(8,128)(2,1)S(1)} %fusion.44), channel_id=1, source_target_pairs={{0,2},{2,4},{4,6},{6,8},{8,10},{10,12},{12,14},{14,0},{1,3},{3,5},... | collective-permute-start | bytes 184328 | tf_op jit(solution)/shard_map/ppermute | solution.py:59
  171.5 1.9 collective-permute-start.12
  173.5 5.3 %collective-permute-start.6 = (bf16[6,8,640]{2,1,0:T(8,128)(2,1)S(1)}, bf16[6,8,640]{2,1,0:T(8,128)(2,1)S(1)}, u32[]{:S(2)}, u32[]{:S(2)}) collective-permute-start(bf16[6,8,640]{2,1,0:T(8,128)(2,1)S(1)} %fusion.43), channel_id=1, source_target_pairs={{0,2},{2,4},{4,6},{6,8},{8,10},{10,12},{12,14},{14,0},{1,3},{3,5},... | collective-permute-start | bytes 184328 | tf_op jit(solution)/shard_map/ppermute | solution.py:59
  178.9 1.9 collective-permute-start.13
  180.8 5.3 %collective-permute-start.7 = (bf16[6,8,640]{2,1,0:T(8,128)(2,1)S(1)}, bf16[6,8,640]{2,1,0:T(8,128)(2,1)S(1)}, u32[]{:S(2)}, u32[]{:S(2)}) collective-permute-start(bf16[6,8,640]{2,1,0:T(8,128)(2,1)S(1)} %fusion.42), channel_id=1, source_target_pairs={{0,2},{2,4},{4,6},{6,8},{8,10},{10,12},{12,14},{14,0},{1,3},{3,5},... | collective-permute-start | bytes 184328 | tf_op jit(solution)/shard_map/ppermute | solution.py:59
  186.2 1.9 collective-permute-start.14
  188.2 5.4 %collective-permute-done.14 = bf16[6,8,640]{2,1,0:T(8,128)(2,1)S(1)} collective-permute-done((bf16[6,8,640]{2,1,0:T(8,128)(2,1)S(1)}, bf16[6,8,640]{2,1,0:T(8,128)(2,1)S(1)}, u32[]{:S(2)}, u32[]{:S(2)}) %collective-permute-start.14) | collective-permute-done | bytes 61472 | tf_op jit(solution)/shard_map/ppermute | solution.py:59
  (89 shorter events, 21.8 us)
Async XLA Ops:
  6.5 56.0 %all-gather.2.cloned.1.call-start = ((), (), s32[]{:S(2)}) async-start(), calls=%async_computation.2 | async-start | bytes 2088960 | tf_op jit(solution)/shard_map/all_gather | solution.py:86
  8.6 13.4 %copy-start.2 = (s32[768]{0:T(1024)S(1)}, s32[768]{0:T(1024)}, u32[]{:S(2)}) copy-start(s32[768]{0:T(1024)} %param.9) | copy-start | bytes 9220
  29.2 33.4 %copy-start = (bf16[8,1,48,1280]{3,2,1,0:T(8,128)(2,1)S(1)}, bf16[8,1,48,1280]{3,2,1,0:T(8,128)(2,1)}, u32[]{:S(2)}) copy-start(bf16[8,1,48,1280]{3,2,1,0:T(8,128)(2,1)} %get-tuple-element.5) | copy-start | bytes 2949124
  65.5 29.2 %all-to-all-start = ((bf16[16,48,96]{2,0,1:T(8,128)(2,1)}), bf16[16,48,96]{2,0,1:T(8,128)(2,1)S(1)}, u32[]{:S(2)}, u32[]{:S(2)}) async-start(bf16[16,48,96]{2,0,1:T(8,128)(2,1)} %copy.47), calls=%async_computation | async-start | bytes 393216 | tf_op jit(solution)/shard_map/all_to_all | solution.py:91
  109.7 22.1 %copy-start.1 = (bf16[8,1,48,1280]{3,2,1,0:T(8,128)(2,1)S(1)}, bf16[8,1,48,1280]{3,2,1,0:T(8,128)(2,1)}, u32[]{:S(2)}) copy-start(bf16[8,1,48,1280]{3,2,1,0:T(8,128)(2,1)} %get-tuple-element.5) | copy-start | bytes 2949124
  112.3 19.2 %all-to-all-start.1 = ((bf16[48,2,768]{2,1,0:T(2,128)(2,1)}), bf16[48,2,768]{2,1,0:T(2,128)(2,1)S(1)}, u32[]{:S(2)}, u32[]{:S(2)}) async-start(bf16[48,2,768]{2,1,0:T(2,128)(2,1)} %reshape.354), calls=%async_computation.1 | async-start | bytes 294912 | tf_op jit(solution)/shard_map/all_to_all | solution.py:134
  134.7 4.7 %collective-permute-start = (bf16[8,6,8,1280]{3,2,1,0:T(8,128)(2,1)}, bf16[8,6,8,1280]{3,2,1,0:T(8,128)(2,1)S(1)}, u32[]{:S(2)}, u32[]{:S(2)}) collective-permute-start(bf16[8,6,8,1280]{3,2,1,0:T(8,128)(2,1)} %dynamic-slice_bitcast_fusion), channel_id=1, source_target_pairs={{0,1},{1,0},{2,3},{3,2},{4,5},{5,4},{6,7},{7,6},{8,9},{9,8},{10,11... | collective-permute-start | bytes 2949128 | tf_op jit(solution)/shard_map/ppermute | solution.py:147
  139.7 6.1 %collective-permute-start.1 = (bf16[6,8,640]{2,1,0:T(8,128)(2,1)S(1)}, bf16[6,8,640]{2,1,0:T(8,128)(2,1)S(1)}, u32[]{:S(2)}, u32[]{:S(2)}) collective-permute-start(bf16[6,8,640]{2,1,0:T(8,128)(2,1)S(1)} %dynamic-slice_bitcast_fusion.2), channel_id=1, source_target_pairs={{0,2},{2,4},{4,6},{6,8},{8,10},{10,12},{12,14},{14,0},{1,3},{3,5},... | collective-permute-start | bytes 184328 | tf_op jit(solution)/shard_map/ppermute | solution.py:59
  142.1 7.3 %collective-permute-start.8 = (bf16[6,8,640]{2,1,0:T(8,128)(2,1)S(1)}, bf16[6,8,640]{2,1,0:T(8,128)(2,1)S(1)}, u32[]{:S(2)}, u32[]{:S(2)}) collective-permute-start(bf16[6,8,640]{2,1,0:T(8,128)(2,1)S(1)} %dynamic-slice_bitcast_fusion.1), channel_id=1, source_target_pairs={{0,14},{2,0},{4,2},{6,4},{8,6},{10,8},{12,10},{14,12},{1,15},{3,1}... | collective-permute-start | bytes 184328 | tf_op jit(solution)/shard_map/ppermute | solution.py:59
  145.9 6.1 %collective-permute-start.2 = (bf16[6,8,640]{2,1,0:T(8,128)(2,1)S(1)}, bf16[6,8,640]{2,1,0:T(8,128)(2,1)S(1)}, u32[]{:S(2)}, u32[]{:S(2)}) collective-permute-start(bf16[6,8,640]{2,1,0:T(8,128)(2,1)S(1)} %fusion.47), channel_id=1, source_target_pairs={{0,2},{2,4},{4,6},{6,8},{8,10},{10,12},{12,14},{14,0},{1,3},{3,5},... | collective-permute-start | bytes 184328 | tf_op jit(solution)/shard_map/ppermute | solution.py:59
  149.5 7.3 %collective-permute-start.9 = (bf16[6,8,640]{2,1,0:T(8,128)(2,1)S(1)}, bf16[6,8,640]{2,1,0:T(8,128)(2,1)S(1)}, u32[]{:S(2)}, u32[]{:S(2)}) collective-permute-start(bf16[6,8,640]{2,1,0:T(8,128)(2,1)S(1)} %fusion.41), channel_id=1, source_target_pairs={{0,14},{2,0},{4,2},{6,4},{8,6},{10,8},{12,10},{14,12},{1,15},{3,1}... | collective-permute-start | bytes 184328 | tf_op jit(solution)/shard_map/ppermute | solution.py:59
  152.0 6.7 %collective-permute-start.3 = (bf16[6,8,640]{2,1,0:T(8,128)(2,1)S(1)}, bf16[6,8,640]{2,1,0:T(8,128)(2,1)S(1)}, u32[]{:S(2)}, u32[]{:S(2)}) collective-permute-start(bf16[6,8,640]{2,1,0:T(8,128)(2,1)S(1)} %fusion.46), channel_id=1, source_target_pairs={{0,2},{2,4},{4,6},{6,8},{8,10},{10,12},{12,14},{14,0},{1,3},{3,5},... | collective-permute-start | bytes 184328 | tf_op jit(solution)/shard_map/ppermute | solution.py:59
  156.8 7.3 %collective-permute-start.10 = (bf16[6,8,640]{2,1,0:T(8,128)(2,1)S(1)}, bf16[6,8,640]{2,1,0:T(8,128)(2,1)S(1)}, u32[]{:S(2)}, u32[]{:S(2)}) collective-permute-start(bf16[6,8,640]{2,1,0:T(8,128)(2,1)S(1)} %fusion.40), channel_id=1, source_target_pairs={{0,14},{2,0},{4,2},{6,4},{8,6},{10,8},{12,10},{14,12},{1,15},{3,1}... | collective-permute-start | bytes 184328 | tf_op jit(solution)/shard_map/ppermute | solution.py:59
  158.8 7.3 %collective-permute-start.4 = (bf16[6,8,640]{2,1,0:T(8,128)(2,1)S(1)}, bf16[6,8,640]{2,1,0:T(8,128)(2,1)S(1)}, u32[]{:S(2)}, u32[]{:S(2)}) collective-permute-start(bf16[6,8,640]{2,1,0:T(8,128)(2,1)S(1)} %fusion.45), channel_id=1, source_target_pairs={{0,2},{2,4},{4,6},{6,8},{8,10},{10,12},{12,14},{14,0},{1,3},{3,5},... | collective-permute-start | bytes 184328 | tf_op jit(solution)/shard_map/ppermute | solution.py:59
  164.2 7.3 %collective-permute-start.11 = (bf16[6,8,640]{2,1,0:T(8,128)(2,1)S(1)}, bf16[6,8,640]{2,1,0:T(8,128)(2,1)S(1)}, u32[]{:S(2)}, u32[]{:S(2)}) collective-permute-start(bf16[6,8,640]{2,1,0:T(8,128)(2,1)S(1)} %fusion.39), channel_id=1, source_target_pairs={{0,14},{2,0},{4,2},{6,4},{8,6},{10,8},{12,10},{14,12},{1,15},{3,1}... | collective-permute-start | bytes 184328 | tf_op jit(solution)/shard_map/ppermute | solution.py:59
  166.1 7.3 %collective-permute-start.5 = (bf16[6,8,640]{2,1,0:T(8,128)(2,1)S(1)}, bf16[6,8,640]{2,1,0:T(8,128)(2,1)S(1)}, u32[]{:S(2)}, u32[]{:S(2)}) collective-permute-start(bf16[6,8,640]{2,1,0:T(8,128)(2,1)S(1)} %fusion.44), channel_id=1, source_target_pairs={{0,2},{2,4},{4,6},{6,8},{8,10},{10,12},{12,14},{14,0},{1,3},{3,5},... | collective-permute-start | bytes 184328 | tf_op jit(solution)/shard_map/ppermute | solution.py:59
  171.5 7.3 %collective-permute-start.12 = (bf16[6,8,640]{2,1,0:T(8,128)(2,1)S(1)}, bf16[6,8,640]{2,1,0:T(8,128)(2,1)S(1)}, u32[]{:S(2)}, u32[]{:S(2)}) collective-permute-start(bf16[6,8,640]{2,1,0:T(8,128)(2,1)S(1)} %fusion.38), channel_id=1, source_target_pairs={{0,14},{2,0},{4,2},{6,4},{8,6},{10,8},{12,10},{14,12},{1,15},{3,1}... | collective-permute-start | bytes 184328 | tf_op jit(solution)/shard_map/ppermute | solution.py:59
  173.5 7.3 %collective-permute-start.6 = (bf16[6,8,640]{2,1,0:T(8,128)(2,1)S(1)}, bf16[6,8,640]{2,1,0:T(8,128)(2,1)S(1)}, u32[]{:S(2)}, u32[]{:S(2)}) collective-permute-start(bf16[6,8,640]{2,1,0:T(8,128)(2,1)S(1)} %fusion.43), channel_id=1, source_target_pairs={{0,2},{2,4},{4,6},{6,8},{8,10},{10,12},{12,14},{14,0},{1,3},{3,5},... | collective-permute-start | bytes 184328 | tf_op jit(solution)/shard_map/ppermute | solution.py:59
  178.9 7.3 %collective-permute-start.13 = (bf16[6,8,640]{2,1,0:T(8,128)(2,1)S(1)}, bf16[6,8,640]{2,1,0:T(8,128)(2,1)S(1)}, u32[]{:S(2)}, u32[]{:S(2)}) collective-permute-start(bf16[6,8,640]{2,1,0:T(8,128)(2,1)S(1)} %fusion.37), channel_id=1, source_target_pairs={{0,14},{2,0},{4,2},{6,4},{8,6},{10,8},{12,10},{14,12},{1,15},{3,1}... | collective-permute-start | bytes 184328 | tf_op jit(solution)/shard_map/ppermute | solution.py:59
  180.8 7.3 %collective-permute-start.7 = (bf16[6,8,640]{2,1,0:T(8,128)(2,1)S(1)}, bf16[6,8,640]{2,1,0:T(8,128)(2,1)S(1)}, u32[]{:S(2)}, u32[]{:S(2)}) collective-permute-start(bf16[6,8,640]{2,1,0:T(8,128)(2,1)S(1)} %fusion.42), channel_id=1, source_target_pairs={{0,2},{2,4},{4,6},{6,8},{8,10},{10,12},{12,14},{14,0},{1,3},{3,5},... | collective-permute-start | bytes 184328 | tf_op jit(solution)/shard_map/ppermute | solution.py:59
  186.2 7.3 %collective-permute-start.14 = (bf16[6,8,640]{2,1,0:T(8,128)(2,1)S(1)}, bf16[6,8,640]{2,1,0:T(8,128)(2,1)S(1)}, u32[]{:S(2)}, u32[]{:S(2)}) collective-permute-start(bf16[6,8,640]{2,1,0:T(8,128)(2,1)S(1)} %fusion.36), channel_id=1, source_target_pairs={{0,14},{2,0},{4,2},{6,4},{8,6},{10,8},{12,10},{14,12},{1,15},{3,1}... | collective-permute-start | bytes 184328 | tf_op jit(solution)/shard_map/ppermute | solution.py:59
Sparse Core Ops, SparseCore 0:
  11.7 50.8 all-gather.1

commit v6 on v4

--- a/solution.py
+++ b/solution.py
@@ -44,6 +44,26 @@
     return stacked.reshape(grid.shape[0], grid.shape[1]).astype(jnp.bfloat16)
 
 
+def core_swap(block):
+    other = lax.ppermute(block, "core", [(0, 1), (1, 0)])
+    first = lax.axis_index("core") == 0
+    return jnp.where(first, block, other), jnp.where(first, other, block)
+
+
+def chip_gather(block):
+    chips = lax.axis_size("chip")
+    core_index = lax.axis_index("core")
+    low, high = core_swap(block)
+    pair_block = jnp.concatenate([low, high], axis=0)
+    share = block.shape[1] // 2
+    half = lax.dynamic_slice_in_dim(pair_block, core_index * share, share, axis=1)
+    sent = jnp.broadcast_to(half[None], (chips,) + half.shape)
+    got = lax.all_to_all(sent, "chip", split_axis=0, concat_axis=0, tiled=True)
+    got = got.reshape((chips * half.shape[0],) + half.shape[1:])
+    low, high = core_swap(got)
+    return jnp.concatenate([low, high], axis=1)
+
+
 def per_device(spectral, legendre, weights, nlon, assignment):
     wave_index = lax.axis_index("wave")
     lev_index = lax.axis_index("chip") * lax.axis_size("core") + lax.axis_index("core")
@@ -62,7 +82,7 @@
     packed_leg = jnp.stack([leg_a, leg_b], axis=1)
     spec_pairs = spectral.reshape(spectral.shape[0], pairs_n, 2, kmax_width)
     packed_spec = jnp.where(front[None], spec_pairs[:, :, 0], spec_pairs[:, :, 1, ::-1])
-    spec_all = lax.all_gather(packed_spec, LEV, axis=0, tiled=True)
+    spec_all = chip_gather(packed_spec)
     columns = spec_all.shape[0]
     four_local = jnp.einsum(
         "pxlk,cpk->pxlc", packed_leg, spec_all, preferred_element_type=jnp.float32

time: 181 us -> 166 us (0.917)
  waiting for transfers between devices: 50.7 us -> 32.5 us
  starting transfers between devices: 24.2 us -> 41.4 us
  between operations: 19.2 us -> 5.6 us
    all_gather x1 -> x0, waiting for transfers between devices: 30.2 us -> none  [per_device(): spec_all = lax.all_gather(packed_spec, LEV, axis=0, tiled=True)]
    ppermute x0 -> x2, starting transfers between devices: none -> 14.8 us  [core_swap(): other = lax.ppermute(block, 'core', [(0, 1), (1, 0)])]
    all_to_all x0 -> x1, waiting for transfers between devices: none -> 10.6 us  [chip_gather(): got = lax.all_to_all(sent, 'chip', split_axis=0, concat_axis=0, tiled=True)]
    all_to_all x0 -> x1, starting transfers between devices: none -> 3.69 us  [chip_gather(): got = lax.all_to_all(sent, 'chip', split_axis=0, concat_axis=0, tiled=True)]
  transfers between devices with their start and end apart: 4 -> 6, of which waited for: 4 -> 5; matrix products, arithmetic and copies ran while one was open for 14% -> 15% of each run, Pallas kernels for 0% -> 0%
where the time goes in v6:
time: 166 us; the launch traced here: 165 us
  starting transfers between devices  41.4 us (25%)
  waiting for transfers between devices  32.5 us (20%)
  blocking collectives  30.2 us (18%)
  other arithmetic  25.7 us (15%)
  local copies, waits for them, and re-layouts  18.6 us (11%)
  matrix products  11.1 us (7%)
  between operations  5.6 us (3%)
    all_to_all x1, blocking collectives, per_device(): lax.all_to_all(pair_sum, 'chip', split_axis=0, concat_axis=0, tiled=True)  30.2 us
    ppermute x2, starting transfers between devices, core_swap(): other = lax.ppermute(block, 'core', [(0, 1), (1, 0)])  14.8 us
    all_to_all x1, waiting for transfers between devices, per_device(): lax.all_to_all(analysed, 'wave', split_axis=0, concat_axis=1, tiled=True)  12.6 us
    all_to_all x1, starting transfers between devices, per_device(): lax.all_to_all(four_local, 'wave', split_axis=1, concat_axis=0, tiled=True)  12.6 us
    all_to_all x1, waiting for transfers between devices, chip_gather(): got = lax.all_to_all(sent, 'chip', split_axis=0, concat_axis=0, tiled=True)  10.6 us
    another operation x3, other arithmetic  7.52 us
    cos x2, other arithmetic, angle_parts(): return (jnp.cos(angle), jnp.sin(angle))  6.37 us
    all_to_all x1, waiting for transfers between devices, per_device(): lax.all_to_all(four_local, 'wave', split_axis=1, concat_axis=0, tiled=True)  5.96 us
  transfers between devices with their start and end apart: 6, of which 5 were waited for; matrix products, arithmetic and copies ran while one was open for 15% of the time, Pallas kernels for 0%

profile of v6, /device:TPU:1, one launch (start us, length us, event | category | flops | bytes accessed | tf_op | source)
XLA Modules:
  0.0 165.1 jit_solution(10058948940865208528)
XLA Ops:
  0.0 1.0 reshape.283
  1.4 0.9 rev.10
  2.3 0.8 dynamic_slice.19
  3.4 12.4 %collective-permute-start = (bf16[6,8,1280]{2,1,0:T(8,128)(2,1)S(1)}, bf16[6,8,1280]{2,1,0:T(8,128)(2,1)S(1)}, u32[]{:S(2)}, u32[]{:S(2)}) collective-permute-start(bf16[6,8,1280]{2,1,0:T(8,128)(2,1)S(1)} %fusion.36), channel_id=1, source_target_pairs={{0,1},{1,0},{2,3},{3,2},{4,5},{5,4},{6,7},{7,6},{8,9},{9,8},{10,11... | collective-permute-start | bytes 368648 | tf_op jit(solution)/shard_map/ppermute | solution.py:48
  15.8 0.9 collective-permute-done
  16.8 1.2 broadcast_in_dim.70
  18.0 3.7 %all-to-all-start = ((bf16[8,12,4,1280]{3,2,1,0:T(4,128)(2,1)}), bf16[8,12,4,1280]{3,2,1,0:T(4,128)(2,1)S(1)}, u32[]{:S(2)}, u32[]{:S(2)}) async-start(bf16[8,12,4,1280]{3,2,1,0:T(4,128)(2,1)} %broadcast_in_dim.70), calls=%async_computation | async-start | bytes 1966080 | tf_op jit(solution)/shard_map/all_to_all | solution.py:61
  21.7 1.3 dynamic_slice.20
  27.6 2.6 %slice_select_fusion = (bf16[8,1,48,1280]{3,2,1,0:T(8,128)(2,1)}, bf16[8,1,48,1280]{3,2,1,0:T(8,128)(2,1)S(1)}) fusion(bf16[8,2,48,1280]{3,2,1,0:T(8,128)(2,1)} %bitcast.71, pred[8,1280]{1,0:T(8,128)(4,1)S(1)} %iota_compare_fusion.2), kind=kLoop, calls=%fused_computation.20 | loop fusion | flops 491520 | bytes 3942400 | tf_op jit(solution)/shard_map/jit(_where)/select_n | solution.py:80
  30.2 1.4 rev.9
  32.5 1.1 fusion.47
  33.6 5.3 %fusion.29 = (f32[128,768]{1,0:T(8,128)S(1)}, f32[128,768]{1,0:T(8,128)S(1)}) fusion(f32[]{:T(128)S(6)} %convert_element_type.70, pred[]{:T(512)S(6)} %lt.129, s32[]{:T(128)S(6)} %select_n.141, s32[768]{0:T(1024)S(1)} %copy-done.4, s32[128]{0:T(128)S(1)} %and_select_fusion.2), kind=kLoop, calls=%fused_computation.55 | loop fusion | flops 1081344 | bytes 790025 | tf_op jit(solution)/shard_map/cos | solution.py:17
  38.9 10.6 %all-to-all-done = bf16[8,12,4,1280]{3,2,1,0:T(4,128)(2,1)S(1)} async-done(((bf16[8,12,4,1280]{3,2,1,0:T(4,128)(2,1)}), bf16[8,12,4,1280]{3,2,1,0:T(4,128)(2,1)S(1)}, u32[]{:S(2)}, u32[]{:S(2)}) %all-to-all-start) | async-done | bytes 983072 | tf_op jit(solution)/shard_map/all_to_all | solution.py:61
  49.5 2.4 %collective-permute-start.1 = (bf16[96,4,1280]{2,0,1:T(8,128)(2,1)S(1)}, bf16[96,4,1280]{2,0,1:T(8,128)(2,1)S(1)}, u32[]{:S(2)}, u32[]{:S(2)}) collective-permute-start(bf16[96,4,1280]{2,0,1:T(8,128)(2,1)S(1)} %copy.36), channel_id=1, source_target_pairs={{0,1},{1,0},{2,3},{3,2},{4,5},{5,4},{6,7},{7,6},{8,9},{9,8},{10,11... | collective-permute-start | bytes 2949128 | tf_op jit(solution)/shard_map/ppermute | solution.py:48
  52.0 4.7 %multiply_subtract_fusion = (bf16[21,128,768]{2,1,0:T(8,128)(2,1)}, bf16[21,128,768]{2,1,0:T(8,128)(2,1)}) fusion(f32[128,768]{1,0:T(8,128)S(1)} %get-tuple-element.30, f32[21,768]{1,0:T(8,128)S(1)} %get-tuple-element.28, f32[128,768]{1,0:T(8,128)S(1)} %get-tuple-element.29, f32[21,768]{1,0:T(8,128)S(1)} %get-tuple-element.27), kind=kLoop, calls=%fused_computation.6 | loop fusion | flops 18579456 | bytes 9172992 | tf_op jit(solution)/shard_map/sub | solution.py:22
  58.5 12.6 %all-to-all-start.1 = ((bf16[16,48,96]{2,0,1:T(8,128)(2,1)}), bf16[16,48,96]{2,0,1:T(8,128)(2,1)S(1)}, u32[]{:S(2)}, u32[]{:S(2)}) async-start(bf16[16,48,96]{2,0,1:T(8,128)(2,1)} %copy.38), calls=%async_computation.1 | async-start | bytes 393216 | tf_op jit(solution)/shard_map/all_to_all | solution.py:90
  71.1 6.6 %fusion = (bf16[2688,768]{1,0:T(8,128)(2,1)}, bf16[2688,768]{1,0:T(8,128)(2,1)}) fusion(bf16[21,128,768]{2,1,0:T(8,128)(2,1)} %get-tuple-element.11, pred[768]{0:T(1024)(128)(4,1)S(1)} %multiply_compare_fusion, pred[2688]{0:T(1024)(128)(4,1)S(1)} %iota_compare_fusion.5, bf16[21,128,768]{2,1,0:T(8,128)(2,1)} %get-tuple-element.12), kind=kLoop, calls=%fused_computation.2 | loop fusion | flops 6193152 | bytes 16518528 | tf_op jit(solution)/shard_map/convert.11
  77.6 1.3 dynamic_slice.22
  79.5 6.0 %all-to-all-done.1 = bf16[16,48,96]{2,0,1:T(8,128)(2,1)S(1)} async-done(((bf16[16,48,96]{2,0,1:T(8,128)(2,1)}), bf16[16,48,96]{2,0,1:T(8,128)(2,1)S(1)}, u32[]{:S(2)}, u32[]{:S(2)}) %all-to-all-start.1) | async-done | bytes 147488 | tf_op jit(solution)/shard_map/all_to_all | solution.py:90
  85.4 0.9 copy.39
  86.3 0.9 reshape_squeeze.3
  87.5 5.2 %fusion.3 = f32[2688,96]{0,1:T(8,128)S(1)} fusion(bf16[2688,768]{1,0:T(8,128)(2,1)} %get-tuple-element.32, bf16[2688,768]{1,0:T(8,128)(2,1)} %get-tuple-element.31, bf16[768,48]{0,1:T(8,128)(2,1)S(1)} %get-tuple-element.33, bf16[768,48]{0,1:T(8,128)(2,1)S(1)} %get-tuple-element.34), kind=kOutput, calls=%fused_computation.8 | convolution fusion | flops 810418176 | bytes 9437184 | tf_op jit(solution)/shard_map/dot_general | solution.py:116
  96.0 4.4 %fusion.2 = f32[1536,96]{0,1:T(8,128)S(1)} fusion(bf16[2688,768]{1,0:T(8,128)(2,1)} %get-tuple-element.32, bf16[2688,768]{1,0:T(8,128)(2,1)} %get-tuple-element.31, bf16[2688,48]{0,1:T(8,128)(2,1)S(1)} %broadcast_select_fusion.3, bf16[2688,48]{0,1:T(8,128)(2,1)S(1)} %convert_element_type.73), kind=kOutput, calls=%fused_computation.7 | convolution fusion | flops 810270720 | bytes 9363456 | tf_op jit(solution)/shard_map/dot_general | solution.py:124
  102.0 1.0 reshape.295
  103.0 5.8 %all-to-all-start.2 = ((bf16[48,2,768]{2,1,0:T(2,128)(2,1)}), bf16[48,2,768]{2,1,0:T(2,128)(2,1)S(1)}, u32[]{:S(2)}, u32[]{:S(2)}) async-start(bf16[48,2,768]{2,1,0:T(2,128)(2,1)} %reshape.295), calls=%async_computation.2 | async-start | bytes 294912 | tf_op jit(solution)/shard_map/all_to_all | solution.py:133
  108.8 12.6 %all-to-all-done.2 = bf16[48,2,768]{2,1,0:T(2,128)(2,1)S(1)} async-done(((bf16[48,2,768]{2,1,0:T(2,128)(2,1)}), bf16[48,2,768]{2,1,0:T(2,128)(2,1)S(1)}, u32[]{:S(2)}, u32[]{:S(2)}) %all-to-all-start.2) | async-done | bytes 147488 | tf_op jit(solution)/shard_map/all_to_all | solution.py:133
  122.6 1.1 copy.43
  123.7 1.0 dynamic-slice_bitcast_fusion
  124.7 4.6 %collective-permute-start.2 = (bf16[8,6,8,1280]{3,2,1,0:T(8,128)(2,1)}, bf16[8,6,8,1280]{3,2,1,0:T(8,128)(2,1)S(1)}, u32[]{:S(2)}, u32[]{:S(2)}) collective-permute-start(bf16[8,6,8,1280]{3,2,1,0:T(8,128)(2,1)} %dynamic-slice_bitcast_fusion), channel_id=1, source_target_pairs={{0,1},{1,0},{2,3},{3,2},{4,5},{5,4},{6,7},{7,6},{8,9},{9,8},{10,11... | collective-permute-start | bytes 2949128 | tf_op jit(solution)/shard_map/ppermute | solution.py:146
  129.3 2.4 %collective-permute-done.2 = bf16[8,6,8,1280]{3,2,1,0:T(8,128)(2,1)S(1)} collective-permute-done((bf16[8,6,8,1280]{3,2,1,0:T(8,128)(2,1)}, bf16[8,6,8,1280]{3,2,1,0:T(8,128)(2,1)S(1)}, u32[]{:S(2)}, u32[]{:S(2)}) %collective-permute-start.2) | collective-permute-done | bytes 983072 | tf_op jit(solution)/shard_map/ppermute | solution.py:146
  131.9 30.2 %all_to_all.40 = bf16[8,6,8,1280]{3,2,1,0:T(8,128)(2,1)S(1)} all-to-all(bf16[8,6,8,1280]{3,2,1,0:T(8,128)(2,1)S(1)} %fusion.8), channel_id=1, replica_groups=mesh['wave'=48,'chip'=8,'core'=2] {'chip'}, dimensions={0} | all-to-all | bytes 1966080 | tf_op jit(solution)/shard_map/all_to_all | solution.py:148
  164.0 1.1 reshape.290
  (60 shorter events, 11.7 us)
Async XLA Ops:
  3.4 13.3 %collective-permute-start = (bf16[6,8,1280]{2,1,0:T(8,128)(2,1)S(1)}, bf16[6,8,1280]{2,1,0:T(8,128)(2,1)S(1)}, u32[]{:S(2)}, u32[]{:S(2)}) collective-permute-start(bf16[6,8,1280]{2,1,0:T(8,128)(2,1)S(1)} %fusion.36), channel_id=1, source_target_pairs={{0,1},{1,0},{2,3},{3,2},{4,5},{5,4},{6,7},{7,6},{8,9},{9,8},{10,11... | collective-permute-start | bytes 368648 | tf_op jit(solution)/shard_map/ppermute | solution.py:48
  18.0 13.8 %copy-start.4 = (s32[768]{0:T(1024)S(1)}, s32[768]{0:T(1024)}, u32[]{:S(2)}) copy-start(s32[768]{0:T(1024)} %param.9) | copy-start | bytes 9220
  18.0 31.4 %all-to-all-start = ((bf16[8,12,4,1280]{3,2,1,0:T(4,128)(2,1)}), bf16[8,12,4,1280]{3,2,1,0:T(4,128)(2,1)S(1)}, u32[]{:S(2)}, u32[]{:S(2)}) async-start(bf16[8,12,4,1280]{3,2,1,0:T(4,128)(2,1)} %broadcast_in_dim.70), calls=%async_computation | async-start | bytes 1966080 | tf_op jit(solution)/shard_map/all_to_all | solution.py:61
  49.5 7.3 %collective-permute-start.1 = (bf16[96,4,1280]{2,0,1:T(8,128)(2,1)S(1)}, bf16[96,4,1280]{2,0,1:T(8,128)(2,1)S(1)}, u32[]{:S(2)}, u32[]{:S(2)}) collective-permute-start(bf16[96,4,1280]{2,0,1:T(8,128)(2,1)S(1)} %copy.36), channel_id=1, source_target_pairs={{0,1},{1,0},{2,3},{3,2},{4,5},{5,4},{6,7},{7,6},{8,9},{9,8},{10,11... | collective-permute-start | bytes 2949128 | tf_op jit(solution)/shard_map/ppermute | solution.py:48
  52.0 5.0 %copy-start = (bf16[8,1,48,1280]{3,2,1,0:T(8,128)(2,1)}, bf16[8,1,48,1280]{3,2,1,0:T(8,128)(2,1)S(1)}, u32[]{:S(2)}) copy-start(bf16[8,1,48,1280]{3,2,1,0:T(8,128)(2,1)S(1)} %broadcast_select_fusion.2) | copy-start | bytes 2949124
  52.0 5.0 %copy-start.2 = (bf16[8,1,48,1280]{3,2,1,0:T(8,128)(2,1)S(1)}, bf16[8,1,48,1280]{3,2,1,0:T(8,128)(2,1)}, u32[]{:S(2)}) copy-start(bf16[8,1,48,1280]{3,2,1,0:T(8,128)(2,1)} %get-tuple-element.5) | copy-start | bytes 2949124
  58.5 26.9 %all-to-all-start.1 = ((bf16[16,48,96]{2,0,1:T(8,128)(2,1)}), bf16[16,48,96]{2,0,1:T(8,128)(2,1)S(1)}, u32[]{:S(2)}, u32[]{:S(2)}) async-start(bf16[16,48,96]{2,0,1:T(8,128)(2,1)} %copy.38), calls=%async_computation.1 | async-start | bytes 393216 | tf_op jit(solution)/shard_map/all_to_all | solution.py:90
  100.4 21.4 %copy-start.1 = (bf16[8,1,48,1280]{3,2,1,0:T(8,128)(2,1)S(1)}, bf16[8,1,48,1280]{3,2,1,0:T(8,128)(2,1)}, u32[]{:S(2)}) copy-start(bf16[8,1,48,1280]{3,2,1,0:T(8,128)(2,1)} %copy-done) | copy-start | bytes 2949124
  100.4 21.4 %copy-start.3 = (bf16[8,1,48,1280]{3,2,1,0:T(8,128)(2,1)S(1)}, bf16[8,1,48,1280]{3,2,1,0:T(8,128)(2,1)}, u32[]{:S(2)}) copy-start(bf16[8,1,48,1280]{3,2,1,0:T(8,128)(2,1)} %get-tuple-element.5) | copy-start | bytes 2949124
  103.0 18.4 %all-to-all-start.2 = ((bf16[48,2,768]{2,1,0:T(2,128)(2,1)}), bf16[48,2,768]{2,1,0:T(2,128)(2,1)S(1)}, u32[]{:S(2)}, u32[]{:S(2)}) async-start(bf16[48,2,768]{2,1,0:T(2,128)(2,1)} %reshape.295), calls=%async_computation.2 | async-start | bytes 294912 | tf_op jit(solution)/shard_map/all_to_all | solution.py:133
  124.7 7.0 %collective-permute-start.2 = (bf16[8,6,8,1280]{3,2,1,0:T(8,128)(2,1)}, bf16[8,6,8,1280]{3,2,1,0:T(8,128)(2,1)S(1)}, u32[]{:S(2)}, u32[]{:S(2)}) collective-permute-start(bf16[8,6,8,1280]{3,2,1,0:T(8,128)(2,1)} %dynamic-slice_bitcast_fusion), channel_id=1, source_target_pairs={{0,1},{1,0},{2,3},{3,2},{4,5},{5,4},{6,7},{7,6},{8,9},{9,8},{10,11... | collective-permute-start | bytes 2949128 | tf_op jit(solution)/shard_map/ppermute | solution.py:146

commit v7 on v6

--- a/solution.py
+++ b/solution.py
@@ -143,10 +143,16 @@
     )
     keep = lax.dynamic_index_in_dim(shares, core_index, axis=1, keepdims=False)
     give = lax.dynamic_index_in_dim(shares, cores - 1 - core_index, axis=1, keepdims=False)
-    got = lax.ppermute(give, "core", [(0, 1), (1, 0)])
-    pair_sum = (keep.astype(jnp.float32) + got.astype(jnp.float32)).astype(jnp.bfloat16)
-    gathered = lax.all_to_all(pair_sum, "chip", split_axis=0, concat_axis=0, tiled=True)
-    summed = jnp.sum(gathered.astype(jnp.float32), axis=0)
+    sums = []
+    step = pairs_n // 2
+    for start in (0, step):
+        got = lax.ppermute(give[:, :, start:start + step], "core", [(0, 1), (1, 0)])
+        pair_sum = (
+            keep[:, :, start:start + step].astype(jnp.float32) + got.astype(jnp.float32)
+        ).astype(jnp.bfloat16)
+        gathered = lax.all_to_all(pair_sum, "chip", split_axis=0, concat_axis=0, tiled=True)
+        sums.append(jnp.sum(gathered.astype(jnp.float32), axis=0))
+    summed = jnp.concatenate(sums, axis=1)
     zero_f = jnp.zeros((), jnp.float32)
     out_a = jnp.where(front[None], summed, zero_f)
     out_b = jnp.where(front[None], zero_f, summed)[:, :, ::-1]

time: 166 us -> 178 us (1.072)
  waiting for transfers between devices: 32.5 us -> 48.7 us
  blocking collectives: 30.2 us -> 19.7 us
  starting transfers between devices: 41.4 us -> 47 us
    all_to_all x0 -> x1, waiting for transfers between devices: none -> 17 us  [per_device(): lax.all_to_all(pair_sum, 'chip', split_axis=0, concat_axis=0, tiled=True)]
    all_to_all x1, blocking collectives: 30.2 us -> 19.7 us  [per_device(): lax.all_to_all(pair_sum, 'chip', split_axis=0, concat_axis=0, tiled=True)]
    all_to_all x0 -> x1, starting transfers between devices: none -> 3.48 us  [per_device(): lax.all_to_all(pair_sum, 'chip', split_axis=0, concat_axis=0, tiled=True)]
    ppermute x1 -> x2, starting transfers between devices: 4.56 us -> 6.52 us  [per_device(): got = lax.ppermute(give[:, :, start:start + step], 'core', [(0, 1), (1, 0)])]
  transfers between devices with their start and end apart: 6 -> 8, of which waited for: 5 -> 6; matrix products, arithmetic and copies ran while one was open for 15% -> 14% of each run, Pallas kernels for 0% -> 0%
where the time goes in v7:
time: 178 us; the launch traced here: 177 us
  waiting for transfers between devices  48.7 us (27%)
  starting transfers between devices  47 us (26%)
  other arithmetic  27.2 us (15%)
  blocking collectives  19.7 us (11%)
  local copies, waits for them, and re-layouts  18 us (10%)
  matrix products  11.1 us (6%)
  between operations  5.62 us (3%)
    all_to_all x1, blocking collectives, per_device(): lax.all_to_all(pair_sum, 'chip', split_axis=0, concat_axis=0, tiled=True)  19.7 us
    all_to_all x1, waiting for transfers between devices, per_device(): lax.all_to_all(pair_sum, 'chip', split_axis=0, concat_axis=0, tiled=True)  17 us
    ppermute x2, starting transfers between devices, core_swap(): other = lax.ppermute(block, 'core', [(0, 1), (1, 0)])  14.8 us
    all_to_all x1, starting transfers between devices, per_device(): lax.all_to_all(four_local, 'wave', split_axis=1, concat_axis=0, tiled=True)  12.6 us
    all_to_all x1, waiting for transfers between devices, per_device(): lax.all_to_all(analysed, 'wave', split_axis=0, concat_axis=1, tiled=True)  12.4 us
    all_to_all x1, waiting for transfers between devices, chip_gather(): got = lax.all_to_all(sent, 'chip', split_axis=0, concat_axis=0, tiled=True)  10.6 us
    another operation x3, other arithmetic  7.53 us
    ppermute x2, starting transfers between devices, per_device(): got = lax.ppermute(give[:, :, start:start + step], 'core', [(0, 1), (1, 0)])  6.52 us
  transfers between devices with their start and end apart: 8, of which 6 were waited for; matrix products, arithmetic and copies ran while one was open for 14% of the time, Pallas kernels for 0%

profile of v7, /device:TPU:1, one launch (start us, length us, event | category | flops | bytes accessed | tf_op | source)
XLA Modules:
  0.0 177.3 jit_solution(7483287669452546346)
XLA Ops:
  0.0 1.0 reshape.303
  3.4 12.4 %collective-permute-start = (bf16[6,8,1280]{2,1,0:T(8,128)(2,1)S(1)}, bf16[6,8,1280]{2,1,0:T(8,128)(2,1)S(1)}, u32[]{:S(2)}, u32[]{:S(2)}) collective-permute-start(bf16[6,8,1280]{2,1,0:T(8,128)(2,1)S(1)} %fusion.35), channel_id=1, source_target_pairs={{0,1},{1,0},{2,3},{3,2},{4,5},{5,4},{6,7},{7,6},{8,9},{9,8},{10,11... | collective-permute-start | bytes 368648 | tf_op jit(solution)/shard_map/ppermute | solution.py:48
  15.8 0.9 collective-permute-done
  16.8 1.2 broadcast_in_dim.70
  18.0 3.7 %all-to-all-start = ((bf16[8,12,4,1280]{3,2,1,0:T(4,128)(2,1)}), bf16[8,12,4,1280]{3,2,1,0:T(4,128)(2,1)S(1)}, u32[]{:S(2)}, u32[]{:S(2)}) async-start(bf16[8,12,4,1280]{3,2,1,0:T(4,128)(2,1)} %broadcast_in_dim.70), calls=%async_computation | async-start | bytes 1966080 | tf_op jit(solution)/shard_map/all_to_all | solution.py:61
  21.7 1.3 dynamic_slice.20
  27.6 2.6 %slice_select_fusion = (bf16[8,1,48,1280]{3,2,1,0:T(8,128)(2,1)}, bf16[8,1,48,1280]{3,2,1,0:T(8,128)(2,1)S(1)}) fusion(bf16[8,2,48,1280]{3,2,1,0:T(8,128)(2,1)} %bitcast.69, pred[8,1280]{1,0:T(8,128)(4,1)S(1)} %iota_compare_fusion.2), kind=kLoop, calls=%fused_computation.17 | loop fusion | flops 491520 | bytes 3942400 | tf_op jit(solution)/shard_map/jit(_where)/select_n | solution.py:80
  30.2 1.4 rev.9
  32.5 1.1 fusion.46
  33.6 5.3 %fusion.28 = (f32[128,768]{1,0:T(8,128)S(1)}, f32[128,768]{1,0:T(8,128)S(1)}) fusion(f32[]{:T(128)S(6)} %convert_element_type.79, pred[]{:T(512)S(6)} %lt.129, s32[]{:T(128)S(6)} %select_n.141, s32[768]{0:T(1024)S(1)} %copy-done.4, s32[128]{0:T(128)S(1)} %and_select_fusion.2), kind=kLoop, calls=%fused_computation.58 | loop fusion | flops 1081344 | bytes 790025 | tf_op jit(solution)/shard_map/cos | solution.py:17
  38.8 10.6 %all-to-all-done = bf16[8,12,4,1280]{3,2,1,0:T(4,128)(2,1)S(1)} async-done(((bf16[8,12,4,1280]{3,2,1,0:T(4,128)(2,1)}), bf16[8,12,4,1280]{3,2,1,0:T(4,128)(2,1)S(1)}, u32[]{:S(2)}, u32[]{:S(2)}) %all-to-all-start) | async-done | bytes 983072 | tf_op jit(solution)/shard_map/all_to_all | solution.py:61
  49.5 2.4 %collective-permute-start.1 = (bf16[96,4,1280]{2,0,1:T(8,128)(2,1)S(1)}, bf16[96,4,1280]{2,0,1:T(8,128)(2,1)S(1)}, u32[]{:S(2)}, u32[]{:S(2)}) collective-permute-start(bf16[96,4,1280]{2,0,1:T(8,128)(2,1)S(1)} %copy.36), channel_id=1, source_target_pairs={{0,1},{1,0},{2,3},{3,2},{4,5},{5,4},{6,7},{7,6},{8,9},{9,8},{10,11... | collective-permute-start | bytes 2949128 | tf_op jit(solution)/shard_map/ppermute | solution.py:48
  52.1 4.7 %multiply_subtract_fusion = (bf16[21,128,768]{2,1,0:T(8,128)(2,1)}, bf16[21,128,768]{2,1,0:T(8,128)(2,1)}) fusion(f32[128,768]{1,0:T(8,128)S(1)} %get-tuple-element.36, f32[21,768]{1,0:T(8,128)S(1)} %get-tuple-element.34, f32[128,768]{1,0:T(8,128)S(1)} %get-tuple-element.35, f32[21,768]{1,0:T(8,128)S(1)} %get-tuple-element.33), kind=kLoop, calls=%fused_computation.6 | loop fusion | flops 18579456 | bytes 9172992 | tf_op jit(solution)/shard_map/sub | solution.py:22
  58.5 12.6 %all-to-all-start.1 = ((bf16[16,48,96]{2,0,1:T(8,128)(2,1)}), bf16[16,48,96]{2,0,1:T(8,128)(2,1)S(1)}, u32[]{:S(2)}, u32[]{:S(2)}) async-start(bf16[16,48,96]{2,0,1:T(8,128)(2,1)} %copy.38), calls=%async_computation.1 | async-start | bytes 393216 | tf_op jit(solution)/shard_map/all_to_all | solution.py:90
  71.1 6.6 %fusion = (bf16[2688,768]{1,0:T(8,128)(2,1)}, bf16[2688,768]{1,0:T(8,128)(2,1)}) fusion(bf16[21,128,768]{2,1,0:T(8,128)(2,1)} %get-tuple-element.17, pred[768]{0:T(1024)(128)(4,1)S(1)} %multiply_compare_fusion, pred[2688]{0:T(1024)(128)(4,1)S(1)} %iota_compare_fusion.5, bf16[21,128,768]{2,1,0:T(8,128)(2,1)} %get-tuple-element.18), kind=kLoop, calls=%fused_computation.2 | loop fusion | flops 6193152 | bytes 16518528 | tf_op jit(solution)/shard_map/convert.10
  77.6 1.3 dynamic_slice.22
  79.5 6.0 %all-to-all-done.1 = bf16[16,48,96]{2,0,1:T(8,128)(2,1)S(1)} async-done(((bf16[16,48,96]{2,0,1:T(8,128)(2,1)}), bf16[16,48,96]{2,0,1:T(8,128)(2,1)S(1)}, u32[]{:S(2)}, u32[]{:S(2)}) %all-to-all-start.1) | async-done | bytes 147488 | tf_op jit(solution)/shard_map/all_to_all | solution.py:90
  86.3 0.9 reshape_squeeze.3
  87.5 5.2 %fusion.3 = f32[2688,96]{0,1:T(8,128)S(1)} fusion(bf16[2688,768]{1,0:T(8,128)(2,1)} %get-tuple-element.38, bf16[2688,768]{1,0:T(8,128)(2,1)} %get-tuple-element.37, bf16[768,48]{0,1:T(8,128)(2,1)S(1)} %get-tuple-element.39, bf16[768,48]{0,1:T(8,128)(2,1)S(1)} %get-tuple-element.40), kind=kOutput, calls=%fused_computation.8 | convolution fusion | flops 810418176 | bytes 9437184 | tf_op jit(solution)/shard_map/dot_general | solution.py:116
  96.0 4.4 %fusion.2 = f32[1536,96]{0,1:T(8,128)S(1)} fusion(bf16[2688,768]{1,0:T(8,128)(2,1)} %get-tuple-element.38, bf16[2688,768]{1,0:T(8,128)(2,1)} %get-tuple-element.37, bf16[2688,48]{0,1:T(8,128)(2,1)S(1)} %broadcast_select_fusion.3, bf16[2688,48]{0,1:T(8,128)(2,1)S(1)} %convert_element_type.82), kind=kOutput, calls=%fused_computation.7 | convolution fusion | flops 810270720 | bytes 9363456 | tf_op jit(solution)/shard_map/dot_general | solution.py:124
  102.1 1.0 reshape.314
  103.0 6.0 %all-to-all-start.2 = ((bf16[48,2,768]{2,1,0:T(2,128)(2,1)}), bf16[48,2,768]{2,1,0:T(2,128)(2,1)S(1)}, u32[]{:S(2)}, u32[]{:S(2)}) async-start(bf16[48,2,768]{2,1,0:T(2,128)(2,1)} %reshape.314), calls=%async_computation.2 | async-start | bytes 294912 | tf_op jit(solution)/shard_map/all_to_all | solution.py:133
  109.0 12.4 %all-to-all-done.2 = bf16[48,2,768]{2,1,0:T(2,128)(2,1)S(1)} async-done(((bf16[48,2,768]{2,1,0:T(2,128)(2,1)}), bf16[48,2,768]{2,1,0:T(2,128)(2,1)S(1)}, u32[]{:S(2)}, u32[]{:S(2)}) %all-to-all-start.2) | async-done | bytes 147488 | tf_op jit(solution)/shard_map/all_to_all | solution.py:133
  122.5 1.1 copy.43
  124.1 4.6 %collective-permute-start.2 = (bf16[8,6,4,1280]{3,2,1,0:T(4,128)(2,1)S(1)}, bf16[8,6,4,1280]{3,2,1,0:T(4,128)(2,1)S(1)}, u32[]{:S(2)}, u32[]{:S(2)}) collective-permute-start(bf16[8,6,4,1280]{3,2,1,0:T(4,128)(2,1)S(1)} %get-tuple-element.15), channel_id=1, source_target_pairs={{0,1},{1,0},{2,3},{3,2},{4,5},{5,4},{6,7},{7,6},{8,9},{9,8},{10,11... | collective-permute-start | bytes 1474568 | tf_op jit(solution)/shard_map/ppermute | solution.py:149
  128.7 1.9 %collective-permute-start.3 = (bf16[8,6,4,1280]{3,2,1,0:T(4,128)(2,1)S(1)}, bf16[8,6,4,1280]{3,2,1,0:T(4,128)(2,1)S(1)}, u32[]{:S(2)}, u32[]{:S(2)}) collective-permute-start(bf16[8,6,4,1280]{3,2,1,0:T(4,128)(2,1)S(1)} %get-tuple-element.16), channel_id=1, source_target_pairs={{0,1},{1,0},{2,3},{3,2},{4,5},{5,4},{6,7},{7,6},{8,9},{9,8},{10,11... | collective-permute-start | bytes 1474568 | tf_op jit(solution)/shard_map/ppermute | solution.py:149
  130.7 1.8 %collective-permute-done.3 = bf16[8,6,4,1280]{3,2,1,0:T(4,128)(2,1)S(1)} collective-permute-done((bf16[8,6,4,1280]{3,2,1,0:T(4,128)(2,1)S(1)}, bf16[8,6,4,1280]{3,2,1,0:T(4,128)(2,1)S(1)}, u32[]{:S(2)}, u32[]{:S(2)}) %collective-permute-start.3) | collective-permute-done | bytes 491552 | tf_op jit(solution)/shard_map/ppermute | solution.py:149
  132.5 1.3 add_convert_fusion.1
  133.8 19.7 %all_to_all.45 = bf16[8,6,4,1280]{3,2,1,0:T(4,128)(2,1)S(1)} all-to-all(bf16[8,6,4,1280]{3,2,1,0:T(4,128)(2,1)S(1)} %get-tuple-element.14), channel_id=1, replica_groups=mesh['wave'=48,'chip'=8,'core'=2] {'chip'}, dimensions={0} | all-to-all | bytes 983040 | tf_op jit(solution)/shard_map/all_to_all | solution.py:153
  153.5 3.5 %all-to-all-start.3 = ((bf16[8,6,4,1280]{3,2,1,0:T(4,128)(2,1)}), bf16[8,6,4,1280]{3,2,1,0:T(4,128)(2,1)S(1)}, u32[]{:S(2)}, u32[]{:S(2)}) async-start(bf16[8,6,4,1280]{3,2,1,0:T(4,128)(2,1)} %get-tuple-element.13), calls=%async_computation.3 | async-start | bytes 983040 | tf_op jit(solution)/shard_map/all_to_all | solution.py:153
  157.2 17.0 %all-to-all-done.3 = bf16[8,6,4,1280]{3,2,1,0:T(4,128)(2,1)S(1)} async-done(((bf16[8,6,4,1280]{3,2,1,0:T(4,128)(2,1)}), bf16[8,6,4,1280]{3,2,1,0:T(4,128)(2,1)S(1)}, u32[]{:S(2)}, u32[]{:S(2)}) %all-to-all-start.3) | async-done | bytes 491552 | tf_op jit(solution)/shard_map/all_to_all | solution.py:153
  176.2 1.1 reshape.310
  (66 shorter events, 14.7 us)
Async XLA Ops:
  3.4 13.3 %collective-permute-start = (bf16[6,8,1280]{2,1,0:T(8,128)(2,1)S(1)}, bf16[6,8,1280]{2,1,0:T(8,128)(2,1)S(1)}, u32[]{:S(2)}, u32[]{:S(2)}) collective-permute-start(bf16[6,8,1280]{2,1,0:T(8,128)(2,1)S(1)} %fusion.35), channel_id=1, source_target_pairs={{0,1},{1,0},{2,3},{3,2},{4,5},{5,4},{6,7},{7,6},{8,9},{9,8},{10,11... | collective-permute-start | bytes 368648 | tf_op jit(solution)/shard_map/ppermute | solution.py:48
  18.0 13.8 %copy-start.4 = (s32[768]{0:T(1024)S(1)}, s32[768]{0:T(1024)}, u32[]{:S(2)}) copy-start(s32[768]{0:T(1024)} %param.9) | copy-start | bytes 9220
  18.0 31.4 %all-to-all-start = ((bf16[8,12,4,1280]{3,2,1,0:T(4,128)(2,1)}), bf16[8,12,4,1280]{3,2,1,0:T(4,128)(2,1)S(1)}, u32[]{:S(2)}, u32[]{:S(2)}) async-start(bf16[8,12,4,1280]{3,2,1,0:T(4,128)(2,1)} %broadcast_in_dim.70), calls=%async_computation | async-start | bytes 1966080 | tf_op jit(solution)/shard_map/all_to_all | solution.py:61
  49.5 7.3 %collective-permute-start.1 = (bf16[96,4,1280]{2,0,1:T(8,128)(2,1)S(1)}, bf16[96,4,1280]{2,0,1:T(8,128)(2,1)S(1)}, u32[]{:S(2)}, u32[]{:S(2)}) collective-permute-start(bf16[96,4,1280]{2,0,1:T(8,128)(2,1)S(1)} %copy.36), channel_id=1, source_target_pairs={{0,1},{1,0},{2,3},{3,2},{4,5},{5,4},{6,7},{7,6},{8,9},{9,8},{10,11... | collective-permute-start | bytes 2949128 | tf_op jit(solution)/shard_map/ppermute | solution.py:48
  52.0 5.0 %copy-start = (bf16[8,1,48,1280]{3,2,1,0:T(8,128)(2,1)}, bf16[8,1,48,1280]{3,2,1,0:T(8,128)(2,1)S(1)}, u32[]{:S(2)}) copy-start(bf16[8,1,48,1280]{3,2,1,0:T(8,128)(2,1)S(1)} %broadcast_select_fusion.2) | copy-start | bytes 2949124
  52.0 5.0 %copy-start.2 = (bf16[8,1,48,1280]{3,2,1,0:T(8,128)(2,1)S(1)}, bf16[8,1,48,1280]{3,2,1,0:T(8,128)(2,1)}, u32[]{:S(2)}) copy-start(bf16[8,1,48,1280]{3,2,1,0:T(8,128)(2,1)} %get-tuple-element.7) | copy-start | bytes 2949124
  58.5 26.9 %all-to-all-start.1 = ((bf16[16,48,96]{2,0,1:T(8,128)(2,1)}), bf16[16,48,96]{2,0,1:T(8,128)(2,1)S(1)}, u32[]{:S(2)}, u32[]{:S(2)}) async-start(bf16[16,48,96]{2,0,1:T(8,128)(2,1)} %copy.38), calls=%async_computation.1 | async-start | bytes 393216 | tf_op jit(solution)/shard_map/all_to_all | solution.py:90
  100.4 21.4 %copy-start.1 = (bf16[8,1,48,1280]{3,2,1,0:T(8,128)(2,1)S(1)}, bf16[8,1,48,1280]{3,2,1,0:T(8,128)(2,1)}, u32[]{:S(2)}) copy-start(bf16[8,1,48,1280]{3,2,1,0:T(8,128)(2,1)} %copy-done) | copy-start | bytes 2949124
  100.4 21.4 %copy-start.3 = (bf16[8,1,48,1280]{3,2,1,0:T(8,128)(2,1)S(1)}, bf16[8,1,48,1280]{3,2,1,0:T(8,128)(2,1)}, u32[]{:S(2)}) copy-start(bf16[8,1,48,1280]{3,2,1,0:T(8,128)(2,1)} %get-tuple-element.7) | copy-start | bytes 2949124
  103.0 18.4 %all-to-all-start.2 = ((bf16[48,2,768]{2,1,0:T(2,128)(2,1)}), bf16[48,2,768]{2,1,0:T(2,128)(2,1)S(1)}, u32[]{:S(2)}, u32[]{:S(2)}) async-start(bf16[48,2,768]{2,1,0:T(2,128)(2,1)} %reshape.314), calls=%async_computation.2 | async-start | bytes 294912 | tf_op jit(solution)/shard_map/all_to_all | solution.py:133
  124.1 6.5 %collective-permute-start.2 = (bf16[8,6,4,1280]{3,2,1,0:T(4,128)(2,1)S(1)}, bf16[8,6,4,1280]{3,2,1,0:T(4,128)(2,1)S(1)}, u32[]{:S(2)}, u32[]{:S(2)}) collective-permute-start(bf16[8,6,4,1280]{3,2,1,0:T(4,128)(2,1)S(1)} %get-tuple-element.15), channel_id=1, source_target_pairs={{0,1},{1,0},{2,3},{3,2},{4,5},{5,4},{6,7},{7,6},{8,9},{9,8},{10,11... | collective-permute-start | bytes 1474568 | tf_op jit(solution)/shard_map/ppermute | solution.py:149
  128.7 3.8 %collective-permute-start.3 = (bf16[8,6,4,1280]{3,2,1,0:T(4,128)(2,1)S(1)}, bf16[8,6,4,1280]{3,2,1,0:T(4,128)(2,1)S(1)}, u32[]{:S(2)}, u32[]{:S(2)}) collective-permute-start(bf16[8,6,4,1280]{3,2,1,0:T(4,128)(2,1)S(1)} %get-tuple-element.16), channel_id=1, source_target_pairs={{0,1},{1,0},{2,3},{3,2},{4,5},{5,4},{6,7},{7,6},{8,9},{9,8},{10,11... | collective-permute-start | bytes 1474568 | tf_op jit(solution)/shard_map/ppermute | solution.py:149
  153.5 20.7 %all-to-all-start.3 = ((bf16[8,6,4,1280]{3,2,1,0:T(4,128)(2,1)}), bf16[8,6,4,1280]{3,2,1,0:T(4,128)(2,1)S(1)}, u32[]{:S(2)}, u32[]{:S(2)}) async-start(bf16[8,6,4,1280]{3,2,1,0:T(4,128)(2,1)} %get-tuple-element.13), calls=%async_computation.3 | async-start | bytes 983040 | tf_op jit(solution)/shard_map/all_to_all | solution.py:153

commit v8 on v6

--- a/solution.py
+++ b/solution.py
@@ -64,6 +64,12 @@
     return jnp.concatenate([low, high], axis=1)
 
 
+def quadratic_blocks(grid):
+    vort, diverg, temper = jnp.split(grid, 3, axis=1)
+    stacked = jnp.concatenate([vort * temper, diverg * temper, vort * diverg], axis=1)
+    return stacked.astype(jnp.bfloat16)
+
+
 def per_device(spectral, legendre, weights, nlon, assignment):
     wave_index = lax.axis_index("wave")
     lev_index = lax.axis_index("chip") * lax.axis_size("core") + lax.axis_index("core")
@@ -84,8 +90,10 @@
     packed_spec = jnp.where(front[None], spec_pairs[:, :, 0], spec_pairs[:, :, 1, ::-1])
     spec_all = chip_gather(packed_spec)
     columns = spec_all.shape[0]
+    levels = columns // 6
+    spec_split = spec_all.reshape(levels, 3, 2, pairs_n, kmax_width)
     four_local = jnp.einsum(
-        "pxlk,cpk->pxlc", packed_leg, spec_all, preferred_element_type=jnp.float32
+        "pxlk,vfrpk->pxlrfv", packed_leg, spec_split, preferred_element_type=jnp.float32
     ).astype(jnp.bfloat16).reshape(slots, lat_band, columns)
     fourier = lax.all_to_all(four_local, "wave", split_axis=1, concat_axis=0, tiled=True)
     mine = fourier.shape[1]
@@ -103,13 +111,12 @@
     table = compose_table(
         half + 1, count, assignment, coarse_cos, coarse_sin, fine_cos, fine_sin, lon_rows
     )
-    pairs = fourier[:, 0, :].reshape(all_slots, half_cols, 2)
     zero_bf = jnp.zeros((), jnp.bfloat16)
     blank = jnp.zeros((all_slots, half_cols), jnp.bfloat16)
     split = jnp.concatenate(
         [
-            jnp.concatenate([pairs[:, :, 0], blank], axis=1),
-            jnp.concatenate([blank, pairs[:, :, 1]], axis=1),
+            jnp.concatenate([fourier[:, 0, :half_cols], blank], axis=1),
+            jnp.concatenate([blank, fourier[:, 0, half_cols:]], axis=1),
         ],
         axis=0,
     )
@@ -118,8 +125,8 @@
     grid_pos = 2.0 * (even + odd)
     grid_neg = 2.0 * (even - odd)
     mirrored = (lon_rows > 0) & (lon_rows < half)
-    prod_pos = quadratic(grid_pos)
-    prod_neg = jnp.where(mirrored[:, None], quadratic(grid_neg), zero_bf)
+    prod_pos = quadratic_blocks(grid_pos)
+    prod_neg = jnp.where(mirrored[:, None], quadratic_blocks(grid_neg), zero_bf)
     both = jnp.concatenate([prod_pos, prod_neg], axis=1)
     total = lax.dot_general(
         table, both, (((0,), (0,)), ((), ())), preferred_element_type=jnp.float32
@@ -127,7 +134,8 @@
     real = total[:all_slots, :half_cols] + total[:all_slots, half_cols:]
     imag = total[all_slots:, :half_cols] - total[all_slots:, half_cols:]
     scale = weight / count.astype(jnp.float32)
-    joined = jnp.stack([real * scale, imag * scale], axis=-1).reshape(all_slots, columns)
+    joined = jnp.stack([real * scale, imag * scale], axis=-1).reshape(all_slots, 3, levels, 2)
+    joined = jnp.transpose(joined, (0, 2, 1, 3)).reshape(all_slots, columns)
     analysed_rows = [joined.astype(jnp.bfloat16)]
     analysed = jnp.stack(analysed_rows, axis=1)
     returned = lax.all_to_all(analysed, "wave", split_axis=0, concat_axis=1, tiled=True)

time: 166 us -> 163 us (0.982)
  matrix products: 11.1 us -> 8.79 us
    dot_general x1, matrix products: 4.43 us -> 1.51 us  [per_device(): lax.dot_general(table, both, (((0,), (0,)), ((), ())), preferred_element_...]
    another operation x7 -> x3, other arithmetic: 8.78 us -> 6.67 us
    unnamed x16 -> x19, local copies, waits for them, and re-layouts: 1.5 us -> 3.4 us
  transfers between devices with their start and end apart: 6 -> 6, of which waited for: 5 -> 5; matrix products, arithmetic and copies ran while one was open for 15% -> 16% of each run, Pallas kernels for 0% -> 0%
where the time goes in v8:
time: 163 us; the launch traced here: 162 us
  starting transfers between devices  41.6 us (26%)
  waiting for transfers between devices  32.5 us (20%)
  blocking collectives  30.2 us (19%)
  other arithmetic  25.6 us (16%)
  local copies, waits for them, and re-layouts  17.9 us (11%)
  matrix products  8.79 us (5%)
  between operations  5.56 us (3%)
    all_to_all x1, blocking collectives, per_device(): lax.all_to_all(pair_sum, 'chip', split_axis=0, concat_axis=0, tiled=True)  30.2 us
    ppermute x2, starting transfers between devices, core_swap(): other = lax.ppermute(block, 'core', [(0, 1), (1, 0)])  14.9 us
    all_to_all x1, waiting for transfers between devices, per_device(): lax.all_to_all(analysed, 'wave', split_axis=0, concat_axis=1, tiled=True)  12.4 us
    all_to_all x1, starting transfers between devices, per_device(): lax.all_to_all(four_local, 'wave', split_axis=1, concat_axis=0, tiled=True)  12.4 us
    all_to_all x1, waiting for transfers between devices, chip_gather(): got = lax.all_to_all(sent, 'chip', split_axis=0, concat_axis=0, tiled=True)  10.6 us
    another operation x3, other arithmetic  6.67 us
    cos x2, other arithmetic, angle_parts(): return (jnp.cos(angle), jnp.sin(angle))  6.37 us
    all_to_all x1, waiting for transfers between devices, per_device(): lax.all_to_all(four_local, 'wave', split_axis=1, concat_axis=0, tiled=True)  6.13 us
  transfers between devices with their start and end apart: 6, of which 5 were waited for; matrix products, arithmetic and copies ran while one was open for 16% of the time, Pallas kernels for 0%

profile of v8, /device:TPU:1, one launch (start us, length us, event | category | flops | bytes accessed | tf_op | source)
XLA Modules:
  0.0 162.2 jit_solution(15335146451135273720)
XLA Ops:
  1.0 1.0 reshape.282
  3.4 12.4 %collective-permute-start = (bf16[6,8,1280]{2,1,0:T(8,128)(2,1)S(1)}, bf16[6,8,1280]{2,1,0:T(8,128)(2,1)S(1)}, u32[]{:S(2)}, u32[]{:S(2)}) collective-permute-start(bf16[6,8,1280]{2,1,0:T(8,128)(2,1)S(1)} %fusion.49), channel_id=1, source_target_pairs={{0,1},{1,0},{2,3},{3,2},{4,5},{5,4},{6,7},{7,6},{8,9},{9,8},{10,11... | collective-permute-start | bytes 368648 | tf_op jit(solution)/shard_map/ppermute | solution.py:48
  15.8 0.9 collective-permute-done
  16.8 1.2 broadcast_in_dim.70
  18.0 3.7 %all-to-all-start = ((bf16[8,12,4,1280]{3,2,1,0:T(4,128)(2,1)}), bf16[8,12,4,1280]{3,2,1,0:T(4,128)(2,1)S(1)}, u32[]{:S(2)}, u32[]{:S(2)}) async-start(bf16[8,12,4,1280]{3,2,1,0:T(4,128)(2,1)} %broadcast_in_dim.70), calls=%async_computation | async-start | bytes 1966080 | tf_op jit(solution)/shard_map/all_to_all | solution.py:61
  21.7 1.3 dynamic_slice.20
  27.5 2.6 %slice_select_fusion = (bf16[8,1,48,1280]{3,2,1,0:T(8,128)(2,1)}, bf16[8,1,48,1280]{3,2,1,0:T(8,128)(2,1)S(1)}) fusion(bf16[8,2,48,1280]{3,2,1,0:T(8,128)(2,1)} %bitcast.69, pred[8,1280]{1,0:T(8,128)(4,1)S(1)} %iota_compare_fusion.2), kind=kLoop, calls=%fused_computation.21 | loop fusion | flops 491520 | bytes 3942400 | tf_op jit(solution)/shard_map/jit(_where)/select_n | solution.py:86
  30.2 1.4 rev.9
  32.5 1.1 fusion.58
  33.6 5.3 %fusion.43 = (f32[128,768]{1,0:T(8,128)S(1)}, f32[128,768]{1,0:T(8,128)S(1)}) fusion(f32[]{:T(128)S(6)} %convert_element_type.70, pred[]{:T(512)S(6)} %lt.129, s32[]{:T(128)S(6)} %select_n.141, s32[768]{0:T(1024)S(1)} %copy-done.6, s32[128]{0:T(128)S(1)} %and_select_fusion.2), kind=kLoop, calls=%fused_computation.61 | loop fusion | flops 1081344 | bytes 790025 | tf_op jit(solution)/shard_map/cos | solution.py:17
  38.9 10.6 %all-to-all-done = bf16[8,12,4,1280]{3,2,1,0:T(4,128)(2,1)S(1)} async-done(((bf16[8,12,4,1280]{3,2,1,0:T(4,128)(2,1)}), bf16[8,12,4,1280]{3,2,1,0:T(4,128)(2,1)S(1)}, u32[]{:S(2)}, u32[]{:S(2)}) %all-to-all-start) | async-done | bytes 983072 | tf_op jit(solution)/shard_map/all_to_all | solution.py:61
  49.4 2.6 %collective-permute-start.1 = (bf16[96,4,1280]{2,1,0:T(4,128)(2,1)S(1)}, bf16[96,4,1280]{2,1,0:T(4,128)(2,1)S(1)}, u32[]{:S(2)}, u32[]{:S(2)}) collective-permute-start(bf16[96,4,1280]{2,1,0:T(4,128)(2,1)S(1)} %bitcast.68), channel_id=1, source_target_pairs={{0,1},{1,0},{2,3},{3,2},{4,5},{5,4},{6,7},{7,6},{8,9},{9,8},{10,11... | collective-permute-start | bytes 2949128 | tf_op jit(solution)/shard_map/ppermute | solution.py:48
  52.1 4.7 %multiply_subtract_fusion = (bf16[21,128,768]{2,1,0:T(8,128)(2,1)}, bf16[21,128,768]{2,1,0:T(8,128)(2,1)}) fusion(f32[128,768]{1,0:T(8,128)S(1)} %get-tuple-element.30, f32[21,768]{1,0:T(8,128)S(1)} %get-tuple-element.28, f32[128,768]{1,0:T(8,128)S(1)} %get-tuple-element.29, f32[21,768]{1,0:T(8,128)S(1)} %get-tuple-element.27), kind=kLoop, calls=%fused_computation.6 | loop fusion | flops 18579456 | bytes 9172992 | tf_op jit(solution)/shard_map/sub | solution.py:22
  56.8 0.9 broadcast_select_fusion.1
  57.8 1.0 pad_maximum_fusion.4
  58.8 1.3 fusion.14
  61.0 12.4 %all-to-all-start.1 = ((bf16[16,48,96]{2,0,1:T(8,128)(2,1)}), bf16[16,48,96]{2,0,1:T(8,128)(2,1)S(1)}, u32[]{:S(2)}, u32[]{:S(2)}) async-start(bf16[16,48,96]{2,0,1:T(8,128)(2,1)} %copy.27), calls=%async_computation.1 | async-start | bytes 393216 | tf_op jit(solution)/shard_map/all_to_all | solution.py:98
  73.4 6.6 %fusion = (bf16[2688,768]{1,0:T(8,128)(2,1)}, bf16[2688,768]{1,0:T(8,128)(2,1)}) fusion(bf16[21,128,768]{2,1,0:T(8,128)(2,1)} %get-tuple-element.11, pred[768]{0:T(1024)(128)(4,1)S(1)} %multiply_compare_fusion, pred[2688]{0:T(1024)(128)(4,1)S(1)} %iota_compare_fusion.5, bf16[21,128,768]{2,1,0:T(8,128)(2,1)} %get-tuple-element.12), kind=kLoop, calls=%fused_computation.2 | loop fusion | flops 6193152 | bytes 16518528 | tf_op jit(solution)/shard_map/convert.11
  79.9 1.3 dynamic_slice.22
  81.8 6.1 %all-to-all-done.1 = bf16[16,48,96]{2,0,1:T(8,128)(2,1)S(1)} async-done(((bf16[16,48,96]{2,0,1:T(8,128)(2,1)}), bf16[16,48,96]{2,0,1:T(8,128)(2,1)S(1)}, u32[]{:S(2)}, u32[]{:S(2)}) %all-to-all-start.1) | async-done | bytes 147488 | tf_op jit(solution)/shard_map/all_to_all | solution.py:98
  88.1 5.3 %fusion.3 = f32[2688,96]{0,1:T(8,128)S(1)} fusion(bf16[2688,768]{1,0:T(8,128)(2,1)} %get-tuple-element.32, bf16[2688,768]{1,0:T(8,128)(2,1)} %get-tuple-element.31, bf16[768,48]{1,0:T(8,128)(2,1)S(1)} %get-tuple-element.26, bf16[768,48]{1,0:T(8,128)(2,1)S(1)} %get-tuple-element.25), kind=kOutput, calls=%fused_computation.8 | convolution fusion | flops 810418176 | bytes 9437184 | tf_op jit(solution)/shard_map/dot_general | solution.py:123
  93.6 1.9 %copy-done = bf16[2688,768]{1,0:T(8,128)(2,1)S(1)} copy-done((bf16[2688,768]{1,0:T(8,128)(2,1)S(1)}, bf16[2688,768]{1,0:T(8,128)(2,1)}, u32[]{:S(2)}) %copy-start) | copy-done | bytes 4128792
  95.5 1.5 fusion.2
  99.1 1.0 reshape.294
  100.1 6.0 %all-to-all-start.2 = ((bf16[48,2,768]{2,1,0:T(2,128)(2,1)}), bf16[48,2,768]{2,1,0:T(2,128)(2,1)S(1)}, u32[]{:S(2)}, u32[]{:S(2)}) async-start(bf16[48,2,768]{2,1,0:T(2,128)(2,1)} %reshape.294), calls=%async_computation.2 | async-start | bytes 294912 | tf_op jit(solution)/shard_map/all_to_all | solution.py:141
  106.1 12.4 %all-to-all-done.2 = bf16[48,2,768]{2,1,0:T(2,128)(2,1)S(1)} async-done(((bf16[48,2,768]{2,1,0:T(2,128)(2,1)}), bf16[48,2,768]{2,1,0:T(2,128)(2,1)S(1)}, u32[]{:S(2)}, u32[]{:S(2)}) %all-to-all-start.2) | async-done | bytes 147488 | tf_op jit(solution)/shard_map/all_to_all | solution.py:141
  119.6 1.1 copy.34
  120.7 1.0 dynamic-slice_bitcast_fusion
  121.8 4.6 %collective-permute-start.2 = (bf16[8,6,8,1280]{3,2,1,0:T(8,128)(2,1)}, bf16[8,6,8,1280]{3,2,1,0:T(8,128)(2,1)S(1)}, u32[]{:S(2)}, u32[]{:S(2)}) collective-permute-start(bf16[8,6,8,1280]{3,2,1,0:T(8,128)(2,1)} %dynamic-slice_bitcast_fusion), channel_id=1, source_target_pairs={{0,1},{1,0},{2,3},{3,2},{4,5},{5,4},{6,7},{7,6},{8,9},{9,8},{10,11... | collective-permute-start | bytes 2949128 | tf_op jit(solution)/shard_map/ppermute | solution.py:154
  126.3 2.4 %collective-permute-done.2 = bf16[8,6,8,1280]{3,2,1,0:T(8,128)(2,1)S(1)} collective-permute-done((bf16[8,6,8,1280]{3,2,1,0:T(8,128)(2,1)}, bf16[8,6,8,1280]{3,2,1,0:T(8,128)(2,1)S(1)}, u32[]{:S(2)}, u32[]{:S(2)}) %collective-permute-start.2) | collective-permute-done | bytes 983072 | tf_op jit(solution)/shard_map/ppermute | solution.py:154
  129.0 30.2 %all_to_all.43 = bf16[8,6,8,1280]{3,2,1,0:T(8,128)(2,1)S(1)} all-to-all(bf16[8,6,8,1280]{3,2,1,0:T(8,128)(2,1)S(1)} %fusion.5), channel_id=1, replica_groups=mesh['wave'=48,'chip'=8,'core'=2] {'chip'}, dimensions={0} | all-to-all | bytes 1966080 | tf_op jit(solution)/shard_map/all_to_all | solution.py:156
  161.0 1.1 reshape.288
  (56 shorter events, 9.8 us)
Async XLA Ops:
  3.4 13.3 %collective-permute-start = (bf16[6,8,1280]{2,1,0:T(8,128)(2,1)S(1)}, bf16[6,8,1280]{2,1,0:T(8,128)(2,1)S(1)}, u32[]{:S(2)}, u32[]{:S(2)}) collective-permute-start(bf16[6,8,1280]{2,1,0:T(8,128)(2,1)S(1)} %fusion.49), channel_id=1, source_target_pairs={{0,1},{1,0},{2,3},{3,2},{4,5},{5,4},{6,7},{7,6},{8,9},{9,8},{10,11... | collective-permute-start | bytes 368648 | tf_op jit(solution)/shard_map/ppermute | solution.py:48
  18.0 13.8 %copy-start.6 = (s32[768]{0:T(1024)S(1)}, s32[768]{0:T(1024)}, u32[]{:S(2)}) copy-start(s32[768]{0:T(1024)} %param.9) | copy-start | bytes 9220
  18.0 31.4 %all-to-all-start = ((bf16[8,12,4,1280]{3,2,1,0:T(4,128)(2,1)}), bf16[8,12,4,1280]{3,2,1,0:T(4,128)(2,1)S(1)}, u32[]{:S(2)}, u32[]{:S(2)}) async-start(bf16[8,12,4,1280]{3,2,1,0:T(4,128)(2,1)} %broadcast_in_dim.70), calls=%async_computation | async-start | bytes 1966080 | tf_op jit(solution)/shard_map/all_to_all | solution.py:61
  49.4 7.4 %collective-permute-start.1 = (bf16[96,4,1280]{2,1,0:T(4,128)(2,1)S(1)}, bf16[96,4,1280]{2,1,0:T(4,128)(2,1)S(1)}, u32[]{:S(2)}, u32[]{:S(2)}) collective-permute-start(bf16[96,4,1280]{2,1,0:T(4,128)(2,1)S(1)} %bitcast.68), channel_id=1, source_target_pairs={{0,1},{1,0},{2,3},{3,2},{4,5},{5,4},{6,7},{7,6},{8,9},{9,8},{10,11... | collective-permute-start | bytes 2949128 | tf_op jit(solution)/shard_map/ppermute | solution.py:48
  52.1 6.7 %copy-start.2 = (bf16[8,1,48,1280]{3,2,1,0:T(8,128)(2,1)}, bf16[8,1,48,1280]{3,2,1,0:T(8,128)(2,1)S(1)}, u32[]{:S(2)}) copy-start(bf16[8,1,48,1280]{3,2,1,0:T(8,128)(2,1)S(1)} %broadcast_select_fusion.2) | copy-start | bytes 2949124
  56.8 1.9 %copy-start.4 = (bf16[8,1,48,1280]{3,2,1,0:T(8,128)(2,1)S(1)}, bf16[8,1,48,1280]{3,2,1,0:T(8,128)(2,1)}, u32[]{:S(2)}) copy-start(bf16[8,1,48,1280]{3,2,1,0:T(8,128)(2,1)} %get-tuple-element.7) | copy-start | bytes 2949124
  61.0 26.9 %all-to-all-start.1 = ((bf16[16,48,96]{2,0,1:T(8,128)(2,1)}), bf16[16,48,96]{2,0,1:T(8,128)(2,1)S(1)}, u32[]{:S(2)}, u32[]{:S(2)}) async-start(bf16[16,48,96]{2,0,1:T(8,128)(2,1)} %copy.27), calls=%async_computation.1 | async-start | bytes 393216 | tf_op jit(solution)/shard_map/all_to_all | solution.py:98
  88.1 5.5 %copy-start.1 = (bf16[2688,768]{1,0:T(8,128)(2,1)S(1)}, bf16[2688,768]{1,0:T(8,128)(2,1)}, u32[]{:S(2)}) copy-start(bf16[2688,768]{1,0:T(8,128)(2,1)} %get-tuple-element.32) | copy-start | bytes 12386308
  93.3 2.2 %copy-start = (bf16[2688,768]{1,0:T(8,128)(2,1)S(1)}, bf16[2688,768]{1,0:T(8,128)(2,1)}, u32[]{:S(2)}) copy-start(bf16[2688,768]{1,0:T(8,128)(2,1)} %get-tuple-element.31) | copy-start | bytes 12386308
  97.0 21.9 %copy-start.3 = (bf16[8,1,48,1280]{3,2,1,0:T(8,128)(2,1)S(1)}, bf16[8,1,48,1280]{3,2,1,0:T(8,128)(2,1)}, u32[]{:S(2)}) copy-start(bf16[8,1,48,1280]{3,2,1,0:T(8,128)(2,1)} %copy-done.2) | copy-start | bytes 2949124
  97.0 21.9 %copy-start.5 = (bf16[8,1,48,1280]{3,2,1,0:T(8,128)(2,1)S(1)}, bf16[8,1,48,1280]{3,2,1,0:T(8,128)(2,1)}, u32[]{:S(2)}) copy-start(bf16[8,1,48,1280]{3,2,1,0:T(8,128)(2,1)} %get-tuple-element.7) | copy-start | bytes 2949124
  100.1 18.4 %all-to-all-start.2 = ((bf16[48,2,768]{2,1,0:T(2,128)(2,1)}), bf16[48,2,768]{2,1,0:T(2,128)(2,1)S(1)}, u32[]{:S(2)}, u32[]{:S(2)}) async-start(bf16[48,2,768]{2,1,0:T(2,128)(2,1)} %reshape.294), calls=%async_computation.2 | async-start | bytes 294912 | tf_op jit(solution)/shard_map/all_to_all | solution.py:141
  121.8 7.0 %collective-permute-start.2 = (bf16[8,6,8,1280]{3,2,1,0:T(8,128)(2,1)}, bf16[8,6,8,1280]{3,2,1,0:T(8,128)(2,1)S(1)}, u32[]{:S(2)}, u32[]{:S(2)}) collective-permute-start(bf16[8,6,8,1280]{3,2,1,0:T(8,128)(2,1)} %dynamic-slice_bitcast_fusion), channel_id=1, source_target_pairs={{0,1},{1,0},{2,3},{3,2},{4,5},{5,4},{6,7},{7,6},{8,9},{9,8},{10,11... | collective-permute-start | bytes 2949128 | tf_op jit(solution)/shard_map/ppermute | solution.py:154
